TPU v7x, 128 devices: a whole 4x4x4 slice. The times are simulated.
128 devices in a mesh: shot: 4 (over z_hi, core), rcv: 32 (over x, y, z_lo).
Axes of the slice: x: 4, y: 4, z: 4 (z_hi: 2, z_lo: 2; z = z_hi * 2 + z_lo), core: 2. Of those that a mesh axis runs over, the one named last changes fastest.
Arguments:
- data: float32 [1, 2, 8192, 1024], P(None, None, 'rcv', 'shot'), may hold values from -6 to 6
- impulse: float32 [1, 2, 8192, 8192], P(None, None, 'rcv'), may hold values from -0.0625 to 0.0625
- wavelet: float32 [1, 2], replicated, may hold values from -96 to 96
- live: int32 [8192, 1024], P('rcv', 'shot'), may hold values from 0 to 1, as said below
Outputs:
- residual: float32 [1, 2, 8192, 1024], P(None, None, 'rcv', 'shot')
- gradient: float32 [1, 2, 8192, 8192], P(None, None, 'rcv', 'shot')
Inputs may be any that keep to these rules, and one draw needn't show every extreme that they name: live[r, s] is 0 where |r - s * 8| is at most a per-shot half gap of 1 to 4 positions, and at scattered dead traces; 1 elsewhere.
All inputs are finite; a program needn't handle non-finite values.
Results may differ from a plain program's by a relative error of at most 0.000084.
Values sent between devices are 32-bit elements; how exact they have to be, the bound alone decides.
No kernel may reach another device: no remote copies, remote signals or barrier semaphores. Data moves between devices by JAX's collectives and lax.ppermute only.
A program may use at most 192 MiB of HBM per device.

v0:
```python
import jax
import jax.numpy as jnp
from jax import lax
from jax.sharding import PartitionSpec as P


def product(left, right, form):
    return jnp.einsum(
        form, left, right, precision=lax.Precision.HIGHEST, preferred_element_type=jnp.float32
    )


def convolve(impulse_cols, panel):
    left_re = impulse_cols[:, 0]
    left_im = impulse_cols[:, 1]
    right_re = panel[:, 0]
    right_im = panel[:, 1]
    out_re = product(left_re, right_re, "frk,fks->frs") - product(left_im, right_im, "frk,fks->frs")
    out_im = product(left_re, right_im, "frk,fks->frs") + product(left_im, right_re, "frk,fks->frs")
    return jnp.stack([out_re, out_im], axis=1)


def correlate(residual, panel, scale):
    res_re = residual[:, 0]
    res_im = residual[:, 1]
    pan_re = panel[:, 0]
    pan_im = panel[:, 1]
    out_re = product(res_re, pan_re, "frs,fks->frk") + product(res_im, pan_im, "frs,fks->frk")
    out_im = product(res_im, pan_re, "frs,fks->frk") - product(res_re, pan_im, "frs,fks->frk")
    return jnp.stack([out_re, out_im], axis=1) * scale


def local(data, impulse, wavelet, live):
    rows_dev = data.shape[2]
    shots_dev = data.shape[3]
    positions = impulse.shape[3]
    total_shots = shots_dev * lax.axis_size("shot")
    spacing = positions // total_shots
    scale = -(total_shots ** (-0.5))
    mask = live.astype(jnp.float32)
    observed = data * mask[None, None]
    row_ids = lax.axis_index("rcv") * rows_dev + lax.broadcasted_iota(
        jnp.int32, (rows_dev, shots_dev), 0
    )
    col_ids = lax.axis_index("shot") * shots_dev + lax.broadcasted_iota(
        jnp.int32, (rows_dev, shots_dev), 1
    )
    source = (row_ids == col_ids * spacing).astype(jnp.float32)
    panel = wavelet[:, :, None, None] * source[None, None] - observed
    predicted = convolve(impulse, lax.all_gather(panel, "rcv", axis=2, tiled=True))
    residual = mask[None, None] * (observed - predicted)
    terms = correlate(residual, lax.all_gather(panel, "rcv", axis=2, tiled=True), scale)
    gradient = lax.psum_scatter(terms, "shot", scatter_dimension=3, tiled=True)
    return (residual, gradient)


def solution(mesh):
    placed = (P(None, None, "rcv", "shot"), P(None, None, "rcv", None), P(), P("rcv", "shot"))
    return jax.shard_map(
        local,
        mesh=mesh,
        in_specs=placed,
        out_specs=(P(None, None, "rcv", "shot"), P(None, None, "rcv", "shot")),
        check_vma=False,
    )
```

profile of v0, /device:TPU:1, one launch (start us, length us, event | category | flops | bytes accessed | tf_op | source)
XLA Modules:
  0.0 620.1 jit_solution(2057710960540643906)
XLA Ops:
  7.2 0.0 all-gather.2.cloned.1.call-start
  7.2 1.0 convert_element_type.10
  8.2 0.1 copy.6
  8.3 1.2 copy.7
  9.6 0.1 compare_convert_fusion
  9.7 1.6 multiply_subtract_fusion
  11.3 0.0 all-gather.2.cloned.1.call-update
  11.3 0.0 reduce-scatter.2.cloned.1.call-start
  11.3 364.2 %all-gather.2.cloned.1.call-done = f32[1,2,8192,256]{2,3,1,0:T(8,128)} async-done(((f32[1,2,256,256]{2,3,1,0:T(8,128)}), f32[1,2,8192,256]{2,3,1,0:T(8,128)}) %all-gather.2.cloned.1.call-update) | async-done | bytes 16777232 | tf_op jit(solution)/shard_map/all_gather | solution.py:50
  375.5 0.0 copy-start
  375.5 21.7 %fusion.4 = f32[256,256]{1,0:T(8,128)S(1)} fusion(f32[1,2,256,8192]{3,2,1,0:T(8,128)} %param.5, f32[1,2,8192,256]{2,3,1,0:T(8,128)} %all-gather.2.cloned.1.call-done), kind=kOutput, calls=%fused_computation.9 | convolution fusion | flops 6442450944 | bytes 17039360 | tf_op jit(solution)/shard_map/frk,fks->frs/dot_general | solution.py:8
  397.2 0.0 copy-done
  397.2 9.6 %fusion.2 = f32[256,256]{1,0:T(8,128)S(1)} fusion(f32[1,2,256,8192]{3,2,1,0:T(8,128)} %param.5, f32[1,2,8192,256]{2,3,1,0:T(8,128)S(1)} %copy-done), kind=kOutput, calls=%fused_computation.7 | convolution fusion | flops 6442450944 | bytes 17039360 | tf_op jit(solution)/shard_map/frk,fks->frs/dot_general | solution.py:8
  406.9 9.7 %fusion.19 = f32[1,1,256,256]{2,3,1,0:T(8,128)S(1)} fusion(f32[256,256]{1,0:T(8,128)S(1)} %fusion.4, f32[1,2,256,8192]{3,2,1,0:T(8,128)} %param.5, f32[1,2,8192,256]{2,3,1,0:T(8,128)S(1)} %copy-done), kind=kOutput, calls=%fused_computation.22 | convolution fusion | flops 6442516480 | bytes 17301504 | tf_op jit(solution)/shard_map/frk,fks->frs/dot_general | solution.py:8
  416.5 9.8 %fusion.25 = f32[1,1,256,256]{2,3,1,0:T(8,128)S(1)} fusion(f32[256,256]{1,0:T(8,128)S(1)} %fusion.2, f32[1,2,256,8192]{3,2,1,0:T(8,128)} %param.5, f32[1,2,8192,256]{2,3,1,0:T(8,128)S(1)} %copy-done), kind=kOutput, calls=%fused_computation.24 | convolution fusion | flops 6442516480 | bytes 17301504 | tf_op jit(solution)/shard_map/frk,fks->frs/dot_general | solution.py:8
  426.4 0.1 fusion.28
  426.5 9.7 %fusion.15 = f32[256,8192]{1,0:T(8,128)} fusion(f32[1,2,8192,256]{2,3,1,0:T(8,128)S(1)} %copy-done, f32[1,2,256,256]{2,3,1,0:T(8,128)S(1)} %fusion.28), kind=kOutput, calls=%fused_computation.20 | convolution fusion | flops 6442450944 | bytes 17039360 | tf_op jit(solution)/shard_map/frs,fks->frk/dot_general | solution.py:8
  436.1 9.6 %fusion.14 = f32[256,8192]{1,0:T(8,128)} fusion(f32[1,2,8192,256]{2,3,1,0:T(8,128)S(1)} %copy-done, f32[1,2,256,256]{2,3,1,0:T(8,128)S(1)} %fusion.28), kind=kOutput, calls=%fused_computation.19 | convolution fusion | flops 6442450944 | bytes 17039360 | tf_op jit(solution)/shard_map/frs,fks->frk/dot_general | solution.py:8
  445.7 11.9 %fusion.1 = f32[1,1,256,8192]{3,2,1,0:T(8,128)} fusion(f32[256,8192]{1,0:T(8,128)} %fusion.15, f32[1,2,8192,256]{2,3,1,0:T(8,128)S(1)} %copy-done, f32[1,2,256,256]{2,3,1,0:T(8,128)S(1)} %fusion.28), kind=kOutput, calls=%fused_computation.4 | convolution fusion | flops 6444548096 | bytes 25427968 | tf_op jit(solution)/shard_map/frs,fks->frk/dot_general | solution.py:8
  457.6 11.8 %fusion = f32[1,1,256,8192]{3,2,1,0:T(8,128)} fusion(f32[256,8192]{1,0:T(8,128)} %fusion.14, f32[1,2,8192,256]{2,3,1,0:T(8,128)S(1)} %copy-done, f32[1,2,256,256]{2,3,1,0:T(8,128)S(1)} %fusion.28), kind=kOutput, calls=%fused_computation.2 | convolution fusion | flops 6444548096 | bytes 25427968 | tf_op jit(solution)/shard_map/frs,fks->frk/dot_general | solution.py:8
  469.4 11.5 %maximum_multiply_fusion = f32[1,2,256,8192]{3,2,1,0:T(8,128)} fusion(f32[1,1,256,8192]{3,2,1,0:T(8,128)} %fusion, f32[1,1,256,8192]{3,2,1,0:T(8,128)} %fusion.1), kind=kLoop, calls=%fused_computation | loop fusion | flops 8388608 | bytes 33554432 | tf_op jit(solution)/shard_map/mul | solution.py:30
  480.9 0.0 reduce-scatter.2.cloned.1.call-update
  480.9 1.0 copy.8
  481.9 131.4 %reduce-scatter.2.cloned.1.call-done = f32[1,2,256,2048]{3,2,1,0:T(8,128)} async-done(((f32[1,2,256,8192]{3,2,1,0:T(8,128)}), f32[1,2,256,2048]{3,2,1,0:T(8,128)}) %reduce-scatter.2.cloned.1.call-update) | async-done | bytes 4194320 | tf_op jit(solution)/shard_map/reduce_scatter | solution.py:53
  (1 shorter events, 0.0 us)
Async XLA Ops:
  7.2 368.4 %all-gather.2.cloned.1.call-start = ((), (), s32[]{:S(2)}) async-start(), calls=%async_computation.1 | async-start | bytes 17301504 | tf_op jit(solution)/shard_map/all_gather | solution.py:50
  11.3 602.0 %reduce-scatter.2.cloned.1.call-start = ((), (), s32[]{:S(2)}) async-start(), calls=%async_computation.2 | async-start | bytes 20971520 | tf_op jit(solution)/shard_map/reduce_scatter | solution.py:53
  375.5 21.7 %copy-start = (f32[1,2,8192,256]{2,3,1,0:T(8,128)S(1)}, f32[1,2,8192,256]{2,3,1,0:T(8,128)}, u32[]{:S(2)}) copy-start(f32[1,2,8192,256]{2,3,1,0:T(8,128)} %all-gather.2.cloned.1.call-done) | copy-start | bytes 50331652
Sparse Core Ops, SparseCore 0:
  11.4 364.0 all-gather.1
  481.0 132.2 reduce-scatter.1
where the time goes:
time: 620 us
  waiting for transfers between devices  496 us (80%)
  matrix products  93.7 us (15%)
  other arithmetic  14.2 us (2%)
  between operations  14.1 us (2%)
    all_gather x1, waiting for transfers between devices, local(): lax.all_gather(panel, 'rcv', axis=2, tiled=True)  364 us
    reduce_scatter x1, waiting for transfers between devices, local(): gradient = lax.psum_scatter(terms, 'shot', scatter_dimension=3, tiled=True)  131 us
    dot_general x8, matrix products, product(): jnp.einsum(form, left, right, precision=lax.Precision.HIGHEST, preferred_...  93.7 us
  transfers between devices with their start and end apart: 2, of which 2 were waited for; matrix products, arithmetic and copies ran while one was open for 0% of the time, Pallas kernels for 0%

commit v1 on v0

v1 whole, which is shorter than its diff:
```python
import jax
import jax.numpy as jnp
from jax import lax
from jax.sharding import Mesh, PartitionSpec as P

RCV = ("x", "y", "zl")
SHOT = ("zh", "c")


def product(left, right, form):
    return jnp.einsum(form, left, right, precision=lax.Precision.HIGH, preferred_element_type=jnp.float32)


def convolve(impulse_cols, panel):
    left_re = impulse_cols[:, 0]
    left_im = impulse_cols[:, 1]
    right_re = panel[:, 0]
    right_im = panel[:, 1]
    out_re = product(left_re, right_re, "frk,fks->frs") - product(left_im, right_im, "frk,fks->frs")
    out_im = product(left_re, right_im, "frk,fks->frs") + product(left_im, right_re, "frk,fks->frs")
    return jnp.stack([out_re, out_im], axis=1)


def correlate(residual, panel, scale):
    res_re = residual[:, 0]
    res_im = residual[:, 1]
    pan_re = panel[:, 0]
    pan_im = panel[:, 1]
    out_re = product(res_re, pan_re, "frs,fks->frk") + product(res_im, pan_im, "frs,fks->frk")
    out_im = product(res_im, pan_re, "frs,fks->frk") - product(res_re, pan_im, "frs,fks->frk")
    return jnp.stack([out_re, out_im], axis=1) * scale


def make_panel(data, wavelet, live, total_shots, positions):
    rows_dev = data.shape[2]
    shots_dev = data.shape[3]
    spacing = positions // total_shots
    mask = live.astype(jnp.float32)
    observed = data * mask[None, None]
    rcv_idx = (lax.axis_index("x") * lax.axis_size("y") + lax.axis_index("y")) * lax.axis_size("zl") + lax.axis_index("zl")
    shot_idx = lax.axis_index("zh") * lax.axis_size("c") + lax.axis_index("c")
    row_ids = rcv_idx * rows_dev + lax.broadcasted_iota(jnp.int32, (rows_dev, shots_dev), 0)
    col_ids = shot_idx * shots_dev + lax.broadcasted_iota(jnp.int32, (rows_dev, shots_dev), 1)
    source = (row_ids == col_ids * spacing).astype(jnp.float32)
    panel = wavelet[:, :, None, None] * source[None, None] - observed
    return mask, observed, panel


def fine_mesh(mesh):
    n_rcv = mesh.shape["rcv"]
    n_shot = mesh.shape["shot"]
    devs = mesh.devices.reshape(2, n_shot // 2, 4, 4, n_rcv // 16)
    return Mesh(devs, ("zh", "c", "x", "y", "zl"))


def local(data, impulse, wavelet, live):
    positions = impulse.shape[3]
    total_shots = data.shape[3] * lax.axis_size(SHOT)
    scale = -(total_shots ** (-0.5))
    mask, observed, panel = make_panel(data, wavelet, live, total_shots, positions)
    g = lax.all_gather(panel, "zl", axis=2, tiled=True)
    g = lax.all_gather(g, "y", axis=2, tiled=True)
    g = lax.all_gather(g, "x", axis=2, tiled=True)
    predicted = convolve(impulse, g)
    residual = mask[None, None] * (observed - predicted)
    terms = correlate(residual, g, scale)
    gradient = lax.psum_scatter(terms, SHOT, scatter_dimension=3, tiled=True)
    return (residual, gradient)


def solution(mesh):
    m = fine_mesh(mesh)
    placed = (P(None, None, RCV, SHOT), P(None, None, RCV, None), P(), P(RCV, SHOT))
    return jax.shard_map(local, mesh=m, in_specs=placed,
                         out_specs=(P(None, None, RCV, SHOT), P(None, None, RCV, SHOT)), check_vma=False)
```

time: 620 us -> 459 us (0.74)
  waiting for transfers between devices: 496 us -> 366 us
  matrix products: 93.7 us -> 62.5 us
    all_gather x1 -> x3, waiting for transfers between devices: 364 us -> 234 us  [the longest x1 156 us: local(): g = lax.all_gather(g, 'x', axis=2, tiled=True)]
    dot_general x8, matrix products: 93.7 us -> 62.5 us  [product(): jnp.einsum(form, left, right, precision=lax.Precision.HIGH, preferred_ele...]
  transfers between devices with their start and end apart: 2 -> 4, of which waited for: 2 -> 4; matrix products, arithmetic and copies ran while one was open for 0% -> 0% of each run, Pallas kernels for 0% -> 0%
where the time goes in v1:
time: 459 us
  waiting for transfers between devices  366 us (80%)
  matrix products  62.5 us (14%)
  other arithmetic  14.2 us (3%)
  between operations  13.9 us (3%)
    all_gather x1, waiting for transfers between devices, local(): g = lax.all_gather(g, 'x', axis=2, tiled=True)  156 us
    reduce_scatter x1, waiting for transfers between devices, local(): gradient = lax.psum_scatter(terms, SHOT, scatter_dimension=3, tiled=True)  132 us
    dot_general x8, matrix products, product(): jnp.einsum(form, left, right, precision=lax.Precision.HIGH, preferred_ele...  62.5 us
    all_gather x1, waiting for transfers between devices, local(): g = lax.all_gather(g, 'y', axis=2, tiled=True)  50.8 us
    all_gather x1, waiting for transfers between devices, local(): g = lax.all_gather(panel, 'zl', axis=2, tiled=True)  27 us
    mul x1, other arithmetic, correlate(): return jnp.stack([out_re, out_im], axis=1) * scale  11.5 us
  transfers between devices with their start and end apart: 4, of which 4 were waited for; matrix products, arithmetic and copies ran while one was open for 0% of the time, Pallas kernels for 0%

profile of v1, /device:TPU:1, one launch (start us, length us, event | category | flops | bytes accessed | tf_op | source)
XLA Modules:
  0.0 459.1 jit_solution(6830394985902087054)
XLA Ops:
  7.2 0.0 all-gather.4.cloned.1.call-start
  7.2 1.0 convert_element_type.10
  8.2 0.1 copy.6
  8.3 1.2 copy.7
  9.6 0.1 compare_convert_fusion
  9.7 1.6 multiply_subtract_fusion
  11.3 0.0 all-gather.4.cloned.1.call-update
  11.3 0.0 all-gather.6.cloned.1.call-start
  11.3 27.0 %all-gather.4.cloned.1.call-done = f32[1,2,512,256]{2,3,1,0:T(8,128)} async-done(((f32[1,2,256,256]{2,3,1,0:T(8,128)}), f32[1,2,512,256]{2,3,1,0:T(8,128)}) %all-gather.4.cloned.1.call-update) | async-done | bytes 1048592 | tf_op jit(solution)/shard_map/all_gather | solution.py:61
  38.3 0.0 all-gather.6.cloned.1.call-update
  38.4 0.0 all-gather.8.cloned.1.call-start
  38.4 50.8 %all-gather.6.cloned.1.call-done = f32[1,2,2048,256]{2,3,1,0:T(8,128)} async-done(((f32[1,2,512,256]{2,3,1,0:T(8,128)}), f32[1,2,2048,256]{2,3,1,0:T(8,128)}) %all-gather.6.cloned.1.call-update) | async-done | bytes 4194320 | tf_op jit(solution)/shard_map/all_gather | solution.py:62
  89.2 0.0 all-gather.8.cloned.1.call-update
  89.3 0.0 reduce-scatter.2.cloned.1.call-start
  89.3 156.0 %all-gather.8.cloned.1.call-done = f32[1,2,8192,256]{2,3,1,0:T(8,128)} async-done(((f32[1,2,2048,256]{2,3,1,0:T(8,128)}), f32[1,2,8192,256]{2,3,1,0:T(8,128)}) %all-gather.8.cloned.1.call-update) | async-done | bytes 16777232 | tf_op jit(solution)/shard_map/all_gather | solution.py:63
  245.3 0.0 copy-start
  245.3 13.3 %fusion.4 = f32[256,256]{1,0:T(8,128)S(1)} fusion(f32[1,2,256,8192]{3,2,1,0:T(8,128)} %param.5, f32[1,2,8192,256]{2,3,1,0:T(8,128)} %all-gather.8.cloned.1.call-done), kind=kOutput, calls=%fused_computation.9 | convolution fusion | flops 3221225472 | bytes 17039360 | tf_op jit(solution)/shard_map/frk,fks->frs/dot_general | solution.py:11
  258.6 0.0 copy-done
  258.6 6.2 %fusion.2 = f32[256,256]{1,0:T(8,128)S(1)} fusion(f32[1,2,256,8192]{3,2,1,0:T(8,128)} %param.5, f32[1,2,8192,256]{2,3,1,0:T(8,128)S(1)} %copy-done), kind=kOutput, calls=%fused_computation.7 | convolution fusion | flops 3221225472 | bytes 17039360 | tf_op jit(solution)/shard_map/frk,fks->frs/dot_general | solution.py:11
  264.9 6.3 %fusion.19 = f32[1,1,256,256]{2,3,1,0:T(8,128)S(1)} fusion(f32[256,256]{1,0:T(8,128)S(1)} %fusion.4, f32[1,2,256,8192]{3,2,1,0:T(8,128)} %param.5, f32[1,2,8192,256]{2,3,1,0:T(8,128)S(1)} %copy-done), kind=kOutput, calls=%fused_computation.22 | convolution fusion | flops 3221291008 | bytes 17301504 | tf_op jit(solution)/shard_map/frk,fks->frs/dot_general | solution.py:11
  271.1 6.3 %fusion.25 = f32[1,1,256,256]{2,3,1,0:T(8,128)S(1)} fusion(f32[256,256]{1,0:T(8,128)S(1)} %fusion.2, f32[1,2,256,8192]{3,2,1,0:T(8,128)} %param.5, f32[1,2,8192,256]{2,3,1,0:T(8,128)S(1)} %copy-done), kind=kOutput, calls=%fused_computation.24 | convolution fusion | flops 3221291008 | bytes 17301504 | tf_op jit(solution)/shard_map/frk,fks->frs/dot_general | solution.py:11
  277.4 0.1 fusion.28
  277.5 6.5 %fusion.15 = f32[256,8192]{1,0:T(8,128)} fusion(f32[1,2,8192,256]{2,3,1,0:T(8,128)S(1)} %copy-done, f32[1,2,256,256]{2,3,1,0:T(8,128)S(1)} %fusion.28), kind=kOutput, calls=%fused_computation.20 | convolution fusion | flops 3221225472 | bytes 17039360 | tf_op jit(solution)/shard_map/frs,fks->frk/dot_general | solution.py:11
  284.0 6.5 %fusion.14 = f32[256,8192]{1,0:T(8,128)} fusion(f32[1,2,8192,256]{2,3,1,0:T(8,128)S(1)} %copy-done, f32[1,2,256,256]{2,3,1,0:T(8,128)S(1)} %fusion.28), kind=kOutput, calls=%fused_computation.19 | convolution fusion | flops 3221225472 | bytes 17039360 | tf_op jit(solution)/shard_map/frs,fks->frk/dot_general | solution.py:11
  290.5 8.7 %fusion.1 = f32[1,1,256,8192]{3,2,1,0:T(8,128)} fusion(f32[256,8192]{1,0:T(8,128)} %fusion.15, f32[1,2,8192,256]{2,3,1,0:T(8,128)S(1)} %copy-done, f32[1,2,256,256]{2,3,1,0:T(8,128)S(1)} %fusion.28), kind=kOutput, calls=%fused_computation.4 | convolution fusion | flops 3223322624 | bytes 25427968 | tf_op jit(solution)/shard_map/frs,fks->frk/dot_general | solution.py:11
  299.2 8.7 %fusion = f32[1,1,256,8192]{3,2,1,0:T(8,128)} fusion(f32[256,8192]{1,0:T(8,128)} %fusion.14, f32[1,2,8192,256]{2,3,1,0:T(8,128)S(1)} %copy-done, f32[1,2,256,256]{2,3,1,0:T(8,128)S(1)} %fusion.28), kind=kOutput, calls=%fused_computation.2 | convolution fusion | flops 3223322624 | bytes 25427968 | tf_op jit(solution)/shard_map/frs,fks->frk/dot_general | solution.py:11
  307.9 11.5 %maximum_multiply_fusion = f32[1,2,256,8192]{3,2,1,0:T(8,128)} fusion(f32[1,1,256,8192]{3,2,1,0:T(8,128)} %fusion, f32[1,1,256,8192]{3,2,1,0:T(8,128)} %fusion.1), kind=kLoop, calls=%fused_computation | loop fusion | flops 8388608 | bytes 33554432 | tf_op jit(solution)/shard_map/mul | solution.py:31
  319.4 0.0 reduce-scatter.2.cloned.1.call-update
  319.4 1.0 copy.8
  320.4 132.1 %reduce-scatter.2.cloned.1.call-done = f32[1,2,256,2048]{3,2,1,0:T(8,128)} async-done(((f32[1,2,256,8192]{3,2,1,0:T(8,128)}), f32[1,2,256,2048]{3,2,1,0:T(8,128)}) %reduce-scatter.2.cloned.1.call-update) | async-done | bytes 4194320 | tf_op jit(solution)/shard_map/reduce_scatter | solution.py:67
  (1 shorter events, 0.0 us)
Async XLA Ops:
  7.2 31.2 %all-gather.4.cloned.1.call-start = ((), (), s32[]{:S(2)}) async-start(), calls=%async_computation.1 | async-start | bytes 1572864 | tf_op jit(solution)/shard_map/all_gather | solution.py:61
  11.3 77.9 %all-gather.6.cloned.1.call-start = ((), (), s32[]{:S(2)}) async-start(), calls=%async_computation.2 | async-start | bytes 5242880 | tf_op jit(solution)/shard_map/all_gather | solution.py:62
  38.4 206.9 %all-gather.8.cloned.1.call-start = ((), (), s32[]{:S(2)}) async-start(), calls=%async_computation.3 | async-start | bytes 20971520 | tf_op jit(solution)/shard_map/all_gather | solution.py:63
  89.3 363.3 %reduce-scatter.2.cloned.1.call-start = ((), (), s32[]{:S(2)}) async-start(), calls=%async_computation.4 | async-start | bytes 20971520 | tf_op jit(solution)/shard_map/reduce_scatter | solution.py:67
  245.3 13.4 %copy-start = (f32[1,2,8192,256]{2,3,1,0:T(8,128)S(1)}, f32[1,2,8192,256]{2,3,1,0:T(8,128)}, u32[]{:S(2)}) copy-start(f32[1,2,8192,256]{2,3,1,0:T(8,128)} %all-gather.8.cloned.1.call-done) | copy-start | bytes 50331652
Sparse Core Ops, SparseCore 0:
  11.4 26.8 all-gather.3
  40.0 49.1 all-gather.5
  90.9 154.3 all-gather.7
  319.5 132.9 reduce-scatter.1

commit v2 on v1

--- a/solution.py
+++ b/solution.py
@@ -53,14 +53,35 @@
     return Mesh(devs, ("zh", "c", "x", "y", "zl"))
 
 
+def ring_gather(block, axis_name, split_axis):
+    n = lax.axis_size(axis_name)
+    i = lax.axis_index(axis_name)
+    fwd = [(s, (s + 1) % n) for s in range(n)]
+    bwd = [(s, (s - 1) % n) for s in range(n)]
+    left = lax.ppermute(block, axis_name, fwd)
+    right = lax.ppermute(block, axis_name, bwd)
+    h = block.shape[split_axis] // 2
+    far_a = lax.ppermute(lax.slice_in_dim(right, 0, h, axis=split_axis), axis_name, bwd)
+    far_b = lax.ppermute(lax.slice_in_dim(left, h, 2 * h, axis=split_axis), axis_name, fwd)
+    far = jnp.concatenate([far_a, far_b], axis=split_axis)
+    by_offset = jnp.stack([block, right, far, left])
+    idx = (jnp.arange(n, dtype=jnp.int32) - i) % n
+    return jnp.take(by_offset, idx, axis=0)
+
+
 def local(data, impulse, wavelet, live):
     positions = impulse.shape[3]
     total_shots = data.shape[3] * lax.axis_size(SHOT)
     scale = -(total_shots ** (-0.5))
     mask, observed, panel = make_panel(data, wavelet, live, total_shots, positions)
     g = lax.all_gather(panel, "zl", axis=2, tiled=True)
-    g = lax.all_gather(g, "y", axis=2, tiled=True)
-    g = lax.all_gather(g, "x", axis=2, tiled=True)
+    g_re = lax.all_gather(g[:, 0], "y", axis=1, tiled=True)
+    g_re = lax.all_gather(g_re, "x", axis=1, tiled=True)
+    f, rows2, cols = g[:, 1].shape
+    gx = ring_gather(g[:, 1], "x", 1)
+    gy = ring_gather(gx, "y", 0)
+    g_im = gy.transpose(2, 1, 0, 3, 4).reshape(f, 16 * rows2, cols)
+    g = jnp.stack([g_re, g_im], axis=1)
     predicted = convolve(impulse, g)
     residual = mask[None, None] * (observed - predicted)
     terms = correlate(residual, g, scale)

time: 459 us -> 434 us (0.946)
  waiting for transfers between devices: 366 us -> 280 us
  local copies, waits for them, and re-layouts: 2.37 us -> 24.7 us
  matrix products: 62.5 us -> 77.8 us
  other arithmetic: 14.2 us -> 27.2 us
  starting transfers between devices: 0.16 us -> 9.52 us
    all_gather x2, waiting for transfers between devices: 207 us -> 31.9 us  [the longest x1 31.9 us: local(): g_re = lax.all_gather(g[:, 0], 'y', axis=1, tiled=True)]
    ppermute x0 -> x8, waiting for transfers between devices: none -> 89.7 us  [the longest x2 53.6 us: ring_gather(): right = lax.ppermute(block, axis_name, bwd)]
    dot_general x8, matrix products: 62.5 us -> 77.8 us  [product(): jnp.einsum(form, left, right, precision=lax.Precision.HIGH, preferred_ele...]
    gather x0 -> x2, local copies, waits for them, and re-layouts: none -> 10 us  [ring_gather(): return jnp.take(by_offset, idx, axis=0)]
    transpose x0 -> x1, local copies, waits for them, and re-layouts: none -> 9.93 us  [local(): g_im = gy.transpose(2, 1, 0, 3, 4).reshape(f, 16 * rows2, cols)]
    ppermute x0 -> x8, starting transfers between devices: none -> 9.36 us  [the longest x2 4.97 us: ring_gather(): lax.ppermute(lax.slice_in_dim(right, 0, h, axis=split_axis), axis_name, bwd)]
    transpose x0 -> x1, other arithmetic: none -> 8.15 us  [local(): g_im = gy.transpose(2, 1, 0, 3, 4).reshape(f, 16 * rows2, cols)]
    another operation x0 -> x4, other arithmetic: none -> 5.79 us  [ring_gather(): by_offset = jnp.stack([block, right, far, left])]
  transfers between devices with their start and end apart: 4 -> 12, of which waited for: 4 -> 9; matrix products, arithmetic and copies ran while one was open for 0% -> 11% of each run, Pallas kernels for 0% -> 0%
where the time goes in v2:
time: 434 us; the launch traced here: 433 us
  waiting for transfers between devices  280 us (65%)
  matrix products  77.8 us (18%)
  other arithmetic  27.2 us (6%)
  local copies, waits for them, and re-layouts  24.7 us (6%)
  between operations  14 us (3%)
  starting transfers between devices  9.52 us (2%)
    reduce_scatter x1, waiting for transfers between devices, local(): gradient = lax.psum_scatter(terms, SHOT, scatter_dimension=3, tiled=True)  131 us
    dot_general x8, matrix products, product(): jnp.einsum(form, left, right, precision=lax.Precision.HIGH, preferred_ele...  77.8 us
    ppermute x2, waiting for transfers between devices, ring_gather(): right = lax.ppermute(block, axis_name, bwd)  53.6 us
    all_gather x1, waiting for transfers between devices, local(): g_re = lax.all_gather(g[:, 0], 'y', axis=1, tiled=True)  31.9 us
    ppermute x2, waiting for transfers between devices, ring_gather(): lax.ppermute(lax.slice_in_dim(right, 0, h, axis=split_axis), axis_name, bwd)  30.2 us
    all_gather x1, waiting for transfers between devices, local(): g = lax.all_gather(panel, 'zl', axis=2, tiled=True)  27 us
    gather x2, local copies, waits for them, and re-layouts, ring_gather(): return jnp.take(by_offset, idx, axis=0)  10 us
    transpose x1, local copies, waits for them, and re-layouts, local(): g_im = gy.transpose(2, 1, 0, 3, 4).reshape(f, 16 * rows2, cols)  9.93 us
  transfers between devices with their start and end apart: 12, of which 9 were waited for; matrix products, arithmetic and copies ran while one was open for 11% of the time, Pallas kernels for 0%

profile of v2, /device:TPU:1, one launch (start us, length us, event | category | flops | bytes accessed | tf_op | source)
XLA Modules:
  0.0 433.3 jit_solution(3456621989293745789)
XLA Ops:
  7.2 1.2 copy.10
  9.7 1.6 multiply_subtract_fusion
  11.3 27.0 %all-gather.6.cloned.1.call-done = f32[1,2,512,256]{2,3,1,0:T(8,128)} async-done(((f32[1,2,256,256]{2,3,1,0:T(8,128)}), f32[1,2,512,256]{2,3,1,0:T(8,128)}) %all-gather.6.cloned.1.call-update) | async-done | bytes 1048592 | tf_op jit(solution)/shard_map/all_gather | solution.py:77
  38.4 2.2 fusion.44
  40.6 31.9 %all-gather.8.cloned.1.call-done = f32[1,1,2048,256]{2,3,1,0:T(8,128)} async-done(((f32[1,1,512,256]{2,3,1,0:T(8,128)}), f32[1,1,2048,256]{2,3,1,0:T(8,128)}) %all-gather.8.cloned.1.call-update) | async-done | bytes 2097168 | tf_op jit(solution)/shard_map/all_gather | solution.py:78
  72.6 2.5 collective-permute-start
  75.0 10.4 %collective-permute-done = f32[1,512,256]{1,2,0:T(8,128)S(1)} collective-permute-done((f32[1,512,256]{1,2,0:T(8,128)S(1)}, f32[1,512,256]{1,2,0:T(8,128)S(1)}, u32[]{:S(2)}, u32[]{:S(2)}) %collective-permute-start) | collective-permute-done | bytes 524320 | tf_op jit(solution)/shard_map/ppermute | solution.py:62
  85.5 3.5 collective-permute-start.1
  89.1 10.9 %collective-permute-done.1 = f32[1,256,256]{1,2,0:T(8,128)S(1)} collective-permute-done((f32[1,256,256]{1,2,0:T(8,128)S(1)}, f32[1,256,256]{1,2,0:T(8,128)S(1)}, u32[]{:S(2)}, u32[]{:S(2)}) %collective-permute-start.1) | collective-permute-done | bytes 262176 | tf_op jit(solution)/shard_map/ppermute | solution.py:64
  100.0 3.6 collective-permute-done.3
  103.7 1.5 maximum_bitcast_fusion.1
  105.2 2.3 gather_fusion
  108.2 1.2 collective-permute-start.6
  109.4 43.1 %collective-permute-done.4 = f32[4,1,512,256]{2,3,0,1:T(8,128)S(1)} collective-permute-done((f32[4,1,512,256]{2,3,0,1:T(8,128)S(1)}, f32[4,1,512,256]{2,3,0,1:T(8,128)S(1)}, u32[]{:S(2)}, u32[]{:S(2)}) %collective-permute-start.4) | collective-permute-done | bytes 2097184 | tf_op jit(solution)/shard_map/ppermute | solution.py:62
  152.5 1.5 collective-permute-start.5
  154.8 19.3 %collective-permute-done.5 = f32[2,1,512,256]{2,3,0,1:T(8,128)S(1)} collective-permute-done((f32[2,1,512,256]{2,3,0,1:T(8,128)S(1)}, f32[2,1,512,256]{2,3,0,1:T(8,128)S(1)}, u32[]{:S(2)}, u32[]{:S(2)}) %collective-permute-start.5) | collective-permute-done | bytes 1048608 | tf_op jit(solution)/shard_map/ppermute | solution.py:64
  174.1 2.4 collective-permute-done.7
  176.6 4.1 maximum_bitcast_fusion
  180.7 7.7 %gather_fusion.1 = f32[4,4,512,256]{2,3,1,0:T(8,128)} fusion(f32[4,4,512,256]{2,3,1,0:T(8,128)} %maximum_bitcast_fusion, s32[1024]{0:T(1024)S(1)} %pad_clamp_fusion), kind=kCustom, calls=%fused_computation.1 | custom fusion | bytes 16777232 | tf_op jit(solution)/shard_map/jit(_take)/gather | solution.py:69
  188.5 8.2 %fusion.6 = f32[1,4,4,512,256]{3,4,1,2,0:T(8,128)} fusion(f32[4,4,512,256]{2,3,1,0:T(8,128)} %gather_fusion.1, pred[4]{0:T(512)(128)(4,1)S(1)} %compare_and_fusion.1), kind=kLoop, calls=%fused_computation.13 | loop fusion | flops 2097152 | bytes 16777220 | tf_op jit(solution)/shard_map/transpose | solution.py:83
  196.6 9.9 %copy.11 = f32[1,4,4,512,256]{4,3,2,1,0:T(8,128)} copy(f32[1,4,4,512,256]{3,4,1,2,0:T(8,128)} %fusion.6) | data formatting | bytes 16777216 | tf_op jit(solution)/shard_map/transpose | solution.py:83
  206.5 11.5 %fusion.4 = f32[256,256]{1,0:T(8,128)S(1)} fusion(f32[8192,256]{1,0:T(8,128)} %bitcast.85, f32[1,2,256,8192]{3,2,1,0:T(8,128)} %param.5), kind=kOutput, calls=%fused_computation.10 | convolution fusion | flops 3221225472 | bytes 17039360 | tf_op jit(solution)/shard_map/frk,fks->frs/dot_general | solution.py:11
  218.1 13.4 %fusion.2 = f32[256,256]{1,0:T(8,128)S(1)} fusion(f32[1,1,8192,256]{2,3,1,0:T(8,128)} %all-gather.10.cloned.1.call-done, f32[1,2,256,8192]{3,2,1,0:T(8,128)} %param.5), kind=kOutput, calls=%fused_computation.8 | convolution fusion | flops 3221225472 | bytes 17039360 | tf_op jit(solution)/shard_map/frk,fks->frs/dot_general | solution.py:11
  231.5 10.0 %fusion.34 = f32[1,1,256,256]{2,3,1,0:T(8,128)S(1)} fusion(f32[256,256]{1,0:T(8,128)S(1)} %fusion.2, f32[8192,256]{1,0:T(8,128)S(1)} %bitcast.86, f32[1,2,256,8192]{3,2,1,0:T(8,128)} %param.5), kind=kOutput, calls=%fused_computation.35 | convolution fusion | flops 3221291008 | bytes 17301504 | tf_op jit(solution)/shard_map/frk,fks->frs/dot_general | solution.py:11
  241.5 6.2 %fusion.26 = f32[1,1,256,256]{2,3,1,0:T(8,128)S(1)} fusion(f32[256,256]{1,0:T(8,128)S(1)} %fusion.4, f32[1,2,256,8192]{3,2,1,0:T(8,128)} %param.5, f32[1,1,8192,256]{2,3,1,0:T(8,128)S(1)} %bitcast.90), kind=kOutput, calls=%fused_computation.33 | convolution fusion | flops 3221291008 | bytes 17301504 | tf_op jit(solution)/shard_map/frk,fks->frs/dot_general | solution.py:11
  247.9 6.6 %fusion.13 = f32[256,8192]{1,0:T(8,128)} fusion(f32[1,1,8192,256]{2,3,1,0:T(8,128)S(1)} %bitcast.90, f32[1,2,256,256]{2,3,1,0:T(8,128)S(1)} %fusion.37), kind=kOutput, calls=%fused_computation.20 | convolution fusion | flops 3221225472 | bytes 17039360 | tf_op jit(solution)/shard_map/frs,fks->frk/dot_general | solution.py:11
  254.5 11.7 %fusion.1 = f32[1,1,256,8192]{3,2,1,0:T(8,128)} fusion(f32[256,8192]{1,0:T(8,128)} %fusion.13, f32[8192,256]{1,0:T(8,128)S(1)} %bitcast.87, f32[1,2,256,256]{2,3,1,0:T(8,128)S(1)} %fusion.37), kind=kOutput, calls=%fused_computation.6 | convolution fusion | flops 3223322624 | bytes 25427968 | tf_op jit(solution)/shard_map/frs,fks->frk/dot_general | solution.py:11
  266.1 6.6 %fusion.11 = f32[256,8192]{1,0:T(8,128)} fusion(f32[1,1,8192,256]{2,3,1,0:T(8,128)S(1)} %bitcast.90, f32[1,2,256,256]{2,3,1,0:T(8,128)S(1)} %fusion.37), kind=kOutput, calls=%fused_computation.18 | convolution fusion | flops 3221225472 | bytes 17039360 | tf_op jit(solution)/shard_map/frs,fks->frk/dot_general | solution.py:11
  272.7 11.8 %fusion = f32[1,1,256,8192]{3,2,1,0:T(8,128)} fusion(f32[256,8192]{1,0:T(8,128)} %fusion.11, f32[8192,256]{1,0:T(8,128)S(1)} %bitcast.88, f32[1,2,256,256]{2,3,1,0:T(8,128)S(1)} %fusion.37), kind=kOutput, calls=%fused_computation.4 | convolution fusion | flops 3223322624 | bytes 25427968 | tf_op jit(solution)/shard_map/frs,fks->frk/dot_general | solution.py:11
  284.5 9.8 %maximum_multiply_fusion = f32[1,2,256,8192]{3,2,1,0:T(8,128)} fusion(f32[1,1,256,8192]{3,2,1,0:T(8,128)} %fusion, f32[1,1,256,8192]{3,2,1,0:T(8,128)S(1)} %bitcast.92), kind=kLoop, calls=%fused_computation.2 | loop fusion | flops 8388608 | bytes 33554432 | tf_op jit(solution)/shard_map/mul | solution.py:31
  294.4 1.0 copy.12
  295.4 131.4 %reduce-scatter.2.cloned.1.call-done = f32[1,2,256,2048]{3,2,1,0:T(8,128)} async-done(((f32[1,2,256,8192]{3,2,1,0:T(8,128)}), f32[1,2,256,2048]{3,2,1,0:T(8,128)}) %reduce-scatter.2.cloned.1.call-update) | async-done | bytes 4194320 | tf_op jit(solution)/shard_map/reduce_scatter | solution.py:88
  (46 shorter events, 3.5 us)
Async XLA Ops:
  7.2 31.2 %all-gather.6.cloned.1.call-start = ((), (), s32[]{:S(2)}) async-start(), calls=%async_computation.1 | async-start | bytes 1572864 | tf_op jit(solution)/shard_map/all_gather | solution.py:77
  11.3 61.2 %all-gather.8.cloned.1.call-start = ((), (), s32[]{:S(2)}) async-start(), calls=%async_computation.3 | async-start | bytes 2621440 | tf_op jit(solution)/shard_map/all_gather | solution.py:78
  40.6 177.5 %all-gather.10.cloned.1.call-start = ((), (), s32[]{:S(2)}) async-start(), calls=%async_computation.4 | async-start | bytes 10485760 | tf_op jit(solution)/shard_map/all_gather | solution.py:79
  72.5 354.3 %reduce-scatter.2.cloned.1.call-start = ((), (), s32[]{:S(2)}) async-start(), calls=%async_computation.2 | async-start | bytes 20971520 | tf_op jit(solution)/shard_map/reduce_scatter | solution.py:88
  72.6 12.9 %collective-permute-start = (f32[1,512,256]{1,2,0:T(8,128)S(1)}, f32[1,512,256]{1,2,0:T(8,128)S(1)}, u32[]{:S(2)}, u32[]{:S(2)}) collective-permute-start(f32[1,512,256]{1,2,0:T(8,128)S(1)} %get-tuple-element.7), channel_id=1, source_target_pairs={{0,24},{8,0},{16,8},{24,16},{1,25},{9,1},{17,9},{25,17},{2,26},{10... | collective-permute-start | bytes 1572872 | tf_op jit(solution)/shard_map/ppermute | solution.py:62
  75.0 13.9 %collective-permute-start.2 = (f32[1,512,256]{1,2,0:T(8,128)S(1)}, f32[1,512,256]{1,2,0:T(8,128)S(1)}, u32[]{:S(2)}, u32[]{:S(2)}) collective-permute-start(f32[1,512,256]{1,2,0:T(8,128)S(1)} %get-tuple-element.7), channel_id=1, source_target_pairs={{0,8},{8,16},{16,24},{24,0},{1,9},{9,17},{17,25},{25,1},{2,10},{10... | collective-permute-start | bytes 1572872 | tf_op jit(solution)/shard_map/ppermute | solution.py:61
  85.5 14.5 %collective-permute-start.1 = (f32[1,256,256]{1,2,0:T(8,128)S(1)}, f32[1,256,256]{1,2,0:T(8,128)S(1)}, u32[]{:S(2)}, u32[]{:S(2)}) collective-permute-start(f32[1,256,256]{1,2,0:T(8,128)S(1)} %slice.46), channel_id=1, source_target_pairs={{0,24},{8,0},{16,8},{24,16},{1,25},{9,1},{17,9},{25,17},{2,26},{10... | collective-permute-start | bytes 786440 | tf_op jit(solution)/shard_map/ppermute | solution.py:64
  89.0 14.7 %collective-permute-start.3 = (f32[1,256,256]{1,2,0:T(8,128)S(1)}, f32[1,256,256]{1,2,0:T(8,128)S(1)}, u32[]{:S(2)}, u32[]{:S(2)}) collective-permute-start(f32[1,256,256]{1,2,0:T(8,128)S(1)} %slice.47), channel_id=1, source_target_pairs={{0,8},{8,16},{16,24},{24,0},{1,9},{9,17},{17,25},{25,1},{2,10},{10... | collective-permute-start | bytes 786440 | tf_op jit(solution)/shard_map/ppermute | solution.py:65
  107.8 44.6 %collective-permute-start.4 = (f32[4,1,512,256]{2,3,0,1:T(8,128)S(1)}, f32[4,1,512,256]{2,3,0,1:T(8,128)S(1)}, u32[]{:S(2)}, u32[]{:S(2)}) collective-permute-start(f32[4,1,512,256]{2,3,0,1:T(8,128)S(1)} %bitcast_select_fusion.1), channel_id=1, source_target_pairs={{0,6},{2,0},{4,2},{6,4},{1,7},{3,1},{5,3},{7,5},{8,14},{10,8},{12,... | collective-permute-start | bytes 6291464 | tf_op jit(solution)/shard_map/ppermute | solution.py:62
  108.2 45.8 %collective-permute-start.6 = (f32[4,1,512,256]{2,3,0,1:T(8,128)S(1)}, f32[4,1,512,256]{2,3,0,1:T(8,128)S(1)}, u32[]{:S(2)}, u32[]{:S(2)}) collective-permute-start(f32[4,1,512,256]{2,3,0,1:T(8,128)S(1)} %bitcast_select_fusion.1), channel_id=1, source_target_pairs={{0,2},{2,4},{4,6},{6,0},{1,3},{3,5},{5,7},{7,1},{8,10},{10,12},{12... | collective-permute-start | bytes 6291464 | tf_op jit(solution)/shard_map/ppermute | solution.py:61
  152.5 21.5 %collective-permute-start.5 = (f32[2,1,512,256]{2,3,0,1:T(8,128)S(1)}, f32[2,1,512,256]{2,3,0,1:T(8,128)S(1)}, u32[]{:S(2)}, u32[]{:S(2)}) collective-permute-start(f32[2,1,512,256]{2,3,0,1:T(8,128)S(1)} %slice.48), channel_id=1, source_target_pairs={{0,6},{2,0},{4,2},{6,4},{1,7},{3,1},{5,3},{7,5},{8,14},{10,8},{12,... | collective-permute-start | bytes 3145736 | tf_op jit(solution)/shard_map/ppermute | solution.py:64
  154.1 22.3 %collective-permute-start.7 = (f32[2,1,512,256]{2,3,0,1:T(8,128)S(1)}, f32[2,1,512,256]{2,3,0,1:T(8,128)S(1)}, u32[]{:S(2)}, u32[]{:S(2)}) collective-permute-start(f32[2,1,512,256]{2,3,0,1:T(8,128)S(1)} %slice.49), channel_id=1, source_target_pairs={{0,2},{2,4},{4,6},{6,0},{1,3},{3,5},{5,7},{7,1},{8,10},{10,12},{12... | collective-permute-start | bytes 3145736 | tf_op jit(solution)/shard_map/ppermute | solution.py:65
  218.1 13.4 %copy-start = (f32[1,4,4,512,256]{4,3,2,1,0:T(8,128)S(1)}, f32[1,4,4,512,256]{4,3,2,1,0:T(8,128)}, u32[]{:S(2)}) copy-start(f32[1,4,4,512,256]{4,3,2,1,0:T(8,128)} %copy.11) | copy-start | bytes 25165828
  218.1 23.4 %slice-start = ((s8[8388608]{0:T(1024)(128)(4,1)}), s8[4194304]{0:T(1024)(128)(4,1)S(1)}, s32[]{:S(2)}) async-start(s8[8388608]{0:T(1024)(128)(4,1)} %bitcast.89), calls=%async_computation.5 | async-start | bytes 8388608
  231.5 10.0 %slice-start.1 = ((s8[8388608]{0:T(1024)(128)(4,1)}), s8[4194304]{0:T(1024)(128)(4,1)S(1)}, s32[]{:S(2)}) async-start(s8[8388608]{0:T(1024)(128)(4,1)} %bitcast.89), calls=%async_computation.6 | async-start | bytes 8388608
  266.1 18.4 %slice-start.2 = ((s8[8388608]{0:T(1024)(128)(4,1)}), s8[4194304]{0:T(1024)(128)(4,1)S(1)}, s32[]{:S(2)}) async-start(s8[8388608]{0:T(1024)(128)(4,1)} %bitcast.91), calls=%async_computation.7 | async-start | bytes 8388608
  272.7 11.8 %slice-start.3 = ((s8[8388608]{0:T(1024)(128)(4,1)}), s8[4194304]{0:T(1024)(128)(4,1)S(1)}, s32[]{:S(2)}) async-start(s8[8388608]{0:T(1024)(128)(4,1)} %bitcast.91), calls=%async_computation.8 | async-start | bytes 8388608
Sparse Core Ops, SparseCore 0:
  11.4 26.8 all-gather.5
  40.7 31.7 all-gather.7
  74.2 89.1 all-gather.9
  294.5 132.2 reduce-scatter.1

commit v3 on v2

--- a/solution.py
+++ b/solution.py
@@ -53,7 +53,7 @@
     return Mesh(devs, ("zh", "c", "x", "y", "zl"))
 
 
-def ring_gather(block, axis_name, split_axis):
+def ring_gather(block, axis_name, axis, split_axis):
     n = lax.axis_size(axis_name)
     i = lax.axis_index(axis_name)
     fwd = [(s, (s + 1) % n) for s in range(n)]
@@ -63,10 +63,21 @@
     h = block.shape[split_axis] // 2
     far_a = lax.ppermute(lax.slice_in_dim(right, 0, h, axis=split_axis), axis_name, bwd)
     far_b = lax.ppermute(lax.slice_in_dim(left, h, 2 * h, axis=split_axis), axis_name, fwd)
-    far = jnp.concatenate([far_a, far_b], axis=split_axis)
-    by_offset = jnp.stack([block, right, far, left])
-    idx = (jnp.arange(n, dtype=jnp.int32) - i) % n
-    return jnp.take(by_offset, idx, axis=0)
+    shape = list(block.shape)
+    shape[axis] = n
+    buf = jnp.zeros(shape, block.dtype)
+
+    def at(part, slot, offset):
+        starts = [0] * len(shape)
+        starts[axis] = slot
+        starts[split_axis] = offset
+        return lax.dynamic_update_slice(buf_ref[0], part, starts)
+
+    buf_ref = [buf]
+    for part, slot, offset in ((block, i, 0), (right, (i + 1) % n, 0), (left, (i + n - 1) % n, 0),
+                               (far_a, (i + 2) % n, 0), (far_b, (i + 2) % n, h)):
+        buf_ref[0] = at(part, slot, offset)
+    return buf_ref[0]
 
 
 def local(data, impulse, wavelet, live):
@@ -78,13 +89,16 @@
     g_re = lax.all_gather(g[:, 0], "y", axis=1, tiled=True)
     g_re = lax.all_gather(g_re, "x", axis=1, tiled=True)
     f, rows2, cols = g[:, 1].shape
-    gx = ring_gather(g[:, 1], "x", 1)
-    gy = ring_gather(gx, "y", 0)
-    g_im = gy.transpose(2, 1, 0, 3, 4).reshape(f, 16 * rows2, cols)
+    gx = ring_gather(g[:, 1].reshape(f, 1, 1, rows2, cols), "x", 1, 3)
+    gy = ring_gather(gx, "y", 2, 1)
+    g_im = gy.reshape(f, 16 * rows2, cols)
     g = jnp.stack([g_re, g_im], axis=1)
     predicted = convolve(impulse, g)
     residual = mask[None, None] * (observed - predicted)
-    terms = correlate(residual, g, scale)
+    lhs_re = jnp.concatenate([residual[:, 0], residual[:, 1]], axis=1) * scale
+    lhs_im = jnp.concatenate([residual[:, 1], -residual[:, 0]], axis=1) * scale
+    terms = product(lhs_re, g[:, 0], "frs,fks->frk") + product(lhs_im, g[:, 1], "frs,fks->frk")
+    terms = terms.reshape(terms.shape[0], 2, terms.shape[1] // 2, terms.shape[2])
     gradient = lax.psum_scatter(terms, SHOT, scatter_dimension=3, tiled=True)
     return (residual, gradient)
 

time: 434 us -> 381 us (0.88)
  other arithmetic: 27.2 us -> 3.14 us
  matrix products: 77.8 us -> 62.7 us
  waiting for transfers between devices: 280 us -> 273 us
  local copies, waits for them, and re-layouts: 24.7 us -> 18.6 us
    dot_general x8 -> x6, matrix products: 77.8 us -> 62.7 us  [product(): jnp.einsum(form, left, right, precision=lax.Precision.HIGH, preferred_ele...]
    ppermute x2, waiting for transfers between devices: 30.2 us -> 19.3 us  [ring_gather(): lax.ppermute(lax.slice_in_dim(right, 0, h, axis=split_axis), axis_name, bwd)]
    gather x2 -> x0, local copies, waits for them, and re-layouts: 10 us -> none  [ring_gather(): return jnp.take(by_offset, idx, axis=0)]
    transpose x1 -> x0, local copies, waits for them, and re-layouts: 9.93 us -> none  [local(): g_im = gy.transpose(2, 1, 0, 3, 4).reshape(f, 16 * rows2, cols)]
    mul x1 -> x0, other arithmetic: 9.81 us -> none  [correlate(): return jnp.stack([out_re, out_im], axis=1) * scale]
    dynamic_update_slice x0 -> x10, local copies, waits for them, and re-layouts: none -> 9.12 us  [at(): return lax.dynamic_update_slice(buf_ref[0], part, starts)]
    transpose x1 -> x0, other arithmetic: 8.15 us -> none  [local(): g_im = gy.transpose(2, 1, 0, 3, 4).reshape(f, 16 * rows2, cols)]
    another operation x4 -> x0, other arithmetic: 5.79 us -> none  [ring_gather(): by_offset = jnp.stack([block, right, far, left])]
  transfers between devices with their start and end apart: 12 -> 12, of which waited for: 9 -> 9; matrix products, arithmetic and copies ran while one was open for 11% -> 4% of each run, Pallas kernels for 0% -> 0%
where the time goes in v3:
time: 381 us; the launch traced here: 380 us
  waiting for transfers between devices  273 us (72%)
  matrix products  62.7 us (16%)
  local copies, waits for them, and re-layouts  18.6 us (5%)
  between operations  14 us (4%)
  starting transfers between devices  9.32 us (2%)
    reduce_scatter x1, waiting for transfers between devices, local(): gradient = lax.psum_scatter(terms, SHOT, scatter_dimension=3, tiled=True)  132 us
    dot_general x6, matrix products, product(): jnp.einsum(form, left, right, precision=lax.Precision.HIGH, preferred_ele...  62.7 us
    ppermute x2, waiting for transfers between devices, ring_gather(): right = lax.ppermute(block, axis_name, bwd)  54 us
    all_gather x1, waiting for transfers between devices, local(): g_re = lax.all_gather(g[:, 0], 'y', axis=1, tiled=True)  31.9 us
    all_gather x1, waiting for transfers between devices, local(): g = lax.all_gather(panel, 'zl', axis=2, tiled=True)  27 us
    ppermute x2, waiting for transfers between devices, ring_gather(): lax.ppermute(lax.slice_in_dim(right, 0, h, axis=split_axis), axis_name, bwd)  19.3 us
    dynamic_update_slice x10, local copies, waits for them, and re-layouts, at(): return lax.dynamic_update_slice(buf_ref[0], part, starts)  9.12 us
    ppermute x2, waiting for transfers between devices, ring_gather(): lax.ppermute(lax.slice_in_dim(left, h, 2 * h, axis=split_axis), axis_name...  8.05 us
  transfers between devices with their start and end apart: 12, of which 9 were waited for; matrix products, arithmetic and copies ran while one was open for 4% of the time, Pallas kernels for 0%

profile of v3, /device:TPU:1, one launch (start us, length us, event | category | flops | bytes accessed | tf_op | source)
XLA Modules:
  0.0 380.3 jit_solution(18161567450763494283)
XLA Ops:
  7.2 1.0 convert_element_type.10
  8.3 2.0 multiply_subtract_fusion
  10.3 27.0 %all-gather.6.cloned.1.call-done = f32[1,2,512,256]{3,2,1,0:T(8,128)} async-done(((f32[1,2,256,256]{3,2,1,0:T(8,128)}), f32[1,2,512,256]{3,2,1,0:T(8,128)}) %all-gather.6.cloned.1.call-update) | async-done | bytes 1048592 | tf_op jit(solution)/shard_map/all_gather | solution.py:88
  37.4 2.2 slice_bitcast_fusion
  39.7 31.9 %all-gather.8.cloned.1.call-done = f32[1,1,2048,256]{3,2,1,0:T(8,128)} async-done(((f32[1,1,512,256]{3,2,1,0:T(8,128)}), f32[1,1,2048,256]{3,2,1,0:T(8,128)}) %all-gather.8.cloned.1.call-update) | async-done | bytes 2097168 | tf_op jit(solution)/shard_map/all_gather | solution.py:89
  71.6 2.5 collective-permute-start
  74.1 10.8 %collective-permute-done = f32[1,1,1,512,256]{4,3,2,1,0:T(8,128)S(1)} collective-permute-done((f32[1,1,1,512,256]{4,3,2,1,0:T(8,128)}, f32[1,1,1,512,256]{4,3,2,1,0:T(8,128)S(1)}, u32[]{:S(2)}, u32[]{:S(2)}) %collective-permute-start) | collective-permute-done | bytes 524320 | tf_op jit(solution)/shard_map/ppermute | solution.py:62
  84.9 3.4 collective-permute-start.2
  88.4 1.1 constant_dynamic-update-slice_fusion.9
  89.7 9.6 %collective-permute-done.2 = f32[1,1,1,256,256]{4,3,2,1,0:T(8,128)S(1)} collective-permute-done((f32[1,1,1,256,256]{4,3,2,1,0:T(8,128)S(1)}, f32[1,1,1,256,256]{4,3,2,1,0:T(8,128)S(1)}, u32[]{:S(2)}, u32[]{:S(2)}) %collective-permute-start.2) | collective-permute-done | bytes 262176 | tf_op jit(solution)/shard_map/ppermute | solution.py:64
  99.4 4.9 %collective-permute-done.3 = f32[1,1,1,256,256]{4,3,2,1,0:T(8,128)S(1)} collective-permute-done((f32[1,1,1,256,256]{4,3,2,1,0:T(8,128)S(1)}, f32[1,1,1,256,256]{4,3,2,1,0:T(8,128)S(1)}, u32[]{:S(2)}, u32[]{:S(2)}) %collective-permute-start.3) | collective-permute-done | bytes 262176 | tf_op jit(solution)/shard_map/ppermute | solution.py:65
  104.3 0.6 collective-permute-start.4
  104.9 0.9 collective-permute-start.5
  105.8 43.3 %collective-permute-done.4 = f32[1,4,1,512,256]{4,3,2,1,0:T(8,128)S(1)} collective-permute-done((f32[1,4,1,512,256]{4,3,2,1,0:T(8,128)S(1)}, f32[1,4,1,512,256]{4,3,2,1,0:T(8,128)S(1)}, u32[]{:S(2)}, u32[]{:S(2)}) %collective-permute-start.4) | collective-permute-done | bytes 2097184 | tf_op jit(solution)/shard_map/ppermute | solution.py:62
  149.1 1.1 slice.46
  150.2 1.7 collective-permute-start.6
  151.9 1.1 slice.47
  153.6 4.2 %broadcast_in_dim.4 = f32[1,4,4,512,256]{4,3,2,1,0:T(8,128)} broadcast(f32[]{:T(128)} %constant.69.clone.1), dimensions={} | broadcast | bytes 8388612 | tf_op jit(solution)/shard_map/broadcast_in_dim | solution.py:68
  157.8 1.5 constant_dynamic-update-slice_fusion.4
  159.3 1.5 constant_dynamic-update-slice_fusion.3
  160.7 1.6 constant_dynamic-update-slice_fusion.2
  162.3 9.7 %collective-permute-done.6 = f32[1,2,1,512,256]{4,3,2,1,0:T(8,128)S(1)} collective-permute-done((f32[1,2,1,512,256]{4,3,2,1,0:T(8,128)}, f32[1,2,1,512,256]{4,3,2,1,0:T(8,128)S(1)}, u32[]{:S(2)}, u32[]{:S(2)}) %collective-permute-start.6) | collective-permute-done | bytes 1048608 | tf_op jit(solution)/shard_map/ppermute | solution.py:64
  172.0 1.1 constant_dynamic-update-slice_fusion.1
  173.0 3.2 collective-permute-done.7
  176.2 2.3 constant_dynamic-update-slice_fusion
  178.5 9.9 %fusion.6 = f32[256,256]{0,1:T(8,128)S(1)} fusion(f32[1,1,8192,256]{3,2,1,0:T(8,128)} %all-gather.10.cloned.1.call-done, f32[1,2,256,8192]{3,2,1,0:T(8,128)} %param.5), kind=kOutput, calls=%fused_computation.7 | convolution fusion | flops 3221225472 | bytes 17039360 | tf_op jit(solution)/shard_map/frk,fks->frs/dot_general | solution.py:11
  188.4 9.1 %fusion.25 = f32[1,1,256,256]{3,2,1,0:T(8,128)S(1)} fusion(f32[256,256]{0,1:T(8,128)S(1)} %fusion.6, f32[8192,256]{1,0:T(8,128)} %bitcast.4, f32[1,2,256,8192]{3,2,1,0:T(8,128)} %param.5), kind=kOutput, calls=%fused_computation.20 | convolution fusion | flops 3221291008 | bytes 17301504 | tf_op jit(solution)/shard_map/frk,fks->frs/dot_general | solution.py:11
  197.5 7.0 %fusion = f32[256,256]{0,1:T(8,128)S(1)} fusion(f32[1,1,8192,256]{3,2,1,0:T(8,128)S(1)} %bitcast.51, f32[1,2,256,8192]{3,2,1,0:T(8,128)} %param.5), kind=kOutput, calls=%fused_computation.1 | convolution fusion | flops 3221225472 | bytes 17039360 | tf_op jit(solution)/shard_map/frk,fks->frs/dot_general | solution.py:11
  204.5 9.0 %fusion.19 = f32[1,1,256,256]{3,2,1,0:T(8,128)S(1)} fusion(f32[256,256]{0,1:T(8,128)S(1)} %fusion, f32[8192,256]{1,0:T(8,128)} %bitcast.4, f32[1,2,256,8192]{3,2,1,0:T(8,128)} %param.5), kind=kOutput, calls=%fused_computation.18 | convolution fusion | flops 3221291008 | bytes 17301504 | tf_op jit(solution)/shard_map/frk,fks->frs/dot_general | solution.py:11
  213.7 11.0 %fusion.8 = f32[512,8192]{1,0:T(8,128)} fusion(f32[1,1,8192,256]{3,2,1,0:T(8,128)S(1)} %bitcast.51, f32[256,256]{1,0:T(8,128)S(1)} %get-tuple-element.5, f32[256,256]{1,0:T(8,128)S(1)} %get-tuple-element.4), kind=kOutput, calls=%fused_computation.9 | convolution fusion | flops 6442713088 | bytes 25690112 | tf_op jit(solution)/shard_map/frs,fks->frk/dot_general | solution.py:11
  224.8 16.7 %convolution_add_fusion = f32[512,8192]{1,0:T(8,128)} fusion(f32[512,8192]{1,0:T(8,128)} %fusion.8, f32[8192,256]{1,0:T(8,128)} %bitcast.4, f32[256,256]{1,0:T(8,128)S(1)} %fusion.39, f32[256,256]{1,0:T(8,128)S(1)} %get-tuple-element.5), kind=kOutput, calls=%fused_computation | convolution fusion | flops 6446907392 | bytes 42467328 | tf_op jit(solution)/shard_map/frs,fks->frk/dot_general | solution.py:11
  241.5 132.2 %reduce-scatter.2.cloned.1.call-done = f32[1,2,256,2048]{3,2,1,0:T(8,128)} async-done(((f32[1,2,256,8192]{3,2,1,0:T(8,128)}), f32[1,2,256,2048]{3,2,1,0:T(8,128)}) %reduce-scatter.2.cloned.1.call-update) | async-done | bytes 4194320 | tf_op jit(solution)/shard_map/reduce_scatter | solution.py:102
  (43 shorter events, 1.5 us)
Async XLA Ops:
  7.2 30.2 %all-gather.6.cloned.1.call-start = ((), (), s32[]{:S(2)}) async-start(), calls=%async_computation.1 | async-start | bytes 1572864 | tf_op jit(solution)/shard_map/all_gather | solution.py:88
  10.3 61.2 %all-gather.8.cloned.1.call-start = ((), (), s32[]{:S(2)}) async-start(), calls=%async_computation.3 | async-start | bytes 2621440 | tf_op jit(solution)/shard_map/all_gather | solution.py:89
  39.6 138.9 %all-gather.10.cloned.1.call-start = ((), (), s32[]{:S(2)}) async-start(), calls=%async_computation.4 | async-start | bytes 10485760 | tf_op jit(solution)/shard_map/all_gather | solution.py:90
  71.6 302.2 %reduce-scatter.2.cloned.1.call-start = ((), (), s32[]{:S(2)}) async-start(), calls=%async_computation.2 | async-start | bytes 20971520 | tf_op jit(solution)/shard_map/reduce_scatter | solution.py:102
  71.6 13.2 %collective-permute-start = (f32[1,1,1,512,256]{4,3,2,1,0:T(8,128)}, f32[1,1,1,512,256]{4,3,2,1,0:T(8,128)S(1)}, u32[]{:S(2)}, u32[]{:S(2)}) collective-permute-start(f32[1,1,1,512,256]{4,3,2,1,0:T(8,128)} %get-tuple-element.2), channel_id=1, source_target_pairs={{0,24},{8,0},{16,8},{24,16},{1,25},{9,1},{17,9},{25,17},{2,26},{10... | collective-permute-start | bytes 1572872 | tf_op jit(solution)/shard_map/ppermute | solution.py:62
  74.1 15.4 %collective-permute-start.1 = (f32[1,1,1,512,256]{4,3,2,1,0:T(8,128)}, f32[1,1,1,512,256]{4,3,2,1,0:T(8,128)S(1)}, u32[]{:S(2)}, u32[]{:S(2)}) collective-permute-start(f32[1,1,1,512,256]{4,3,2,1,0:T(8,128)} %get-tuple-element.2), channel_id=1, source_target_pairs={{0,8},{8,16},{16,24},{24,0},{1,9},{9,17},{17,25},{25,1},{2,10},{10... | collective-permute-start | bytes 1572872 | tf_op jit(solution)/shard_map/ppermute | solution.py:61
  84.9 14.5 %collective-permute-start.2 = (f32[1,1,1,256,256]{4,3,2,1,0:T(8,128)S(1)}, f32[1,1,1,256,256]{4,3,2,1,0:T(8,128)S(1)}, u32[]{:S(2)}, u32[]{:S(2)}) collective-permute-start(f32[1,1,1,256,256]{4,3,2,1,0:T(8,128)S(1)} %slice.44), channel_id=1, source_target_pairs={{0,24},{8,0},{16,8},{24,16},{1,25},{9,1},{17,9},{25,17},{2,26},{10... | collective-permute-start | bytes 786440 | tf_op jit(solution)/shard_map/ppermute | solution.py:64
  89.6 14.7 %collective-permute-start.3 = (f32[1,1,1,256,256]{4,3,2,1,0:T(8,128)S(1)}, f32[1,1,1,256,256]{4,3,2,1,0:T(8,128)S(1)}, u32[]{:S(2)}, u32[]{:S(2)}) collective-permute-start(f32[1,1,1,256,256]{4,3,2,1,0:T(8,128)S(1)} %slice.45), channel_id=1, source_target_pairs={{0,8},{8,16},{16,24},{24,0},{1,9},{9,17},{17,25},{25,1},{2,10},{10... | collective-permute-start | bytes 786440 | tf_op jit(solution)/shard_map/ppermute | solution.py:65
  104.3 44.8 %collective-permute-start.4 = (f32[1,4,1,512,256]{4,3,2,1,0:T(8,128)S(1)}, f32[1,4,1,512,256]{4,3,2,1,0:T(8,128)S(1)}, u32[]{:S(2)}, u32[]{:S(2)}) collective-permute-start(f32[1,4,1,512,256]{4,3,2,1,0:T(8,128)S(1)} %constant_dynamic-update-slice_fusion.5), channel_id=1, source_target_pairs={{0,6},{2,0},{4,2},{6,4},{1,7},{3,1},{5,3},{7,5},{8,14},{10,8},{12,... | collective-permute-start | bytes 6291464 | tf_op jit(solution)/shard_map/ppermute | solution.py:62
  104.9 47.0 %collective-permute-start.5 = (f32[1,4,1,512,256]{4,3,2,1,0:T(8,128)S(1)}, f32[1,4,1,512,256]{4,3,2,1,0:T(8,128)S(1)}, u32[]{:S(2)}, u32[]{:S(2)}) collective-permute-start(f32[1,4,1,512,256]{4,3,2,1,0:T(8,128)S(1)} %constant_dynamic-update-slice_fusion.5), channel_id=1, source_target_pairs={{0,2},{2,4},{4,6},{6,0},{1,3},{3,5},{5,7},{7,1},{8,10},{10,12},{12... | collective-permute-start | bytes 6291464 | tf_op jit(solution)/shard_map/ppermute | solution.py:61
  149.1 2.8 copy-start
  150.2 21.7 %collective-permute-start.6 = (f32[1,2,1,512,256]{4,3,2,1,0:T(8,128)}, f32[1,2,1,512,256]{4,3,2,1,0:T(8,128)S(1)}, u32[]{:S(2)}, u32[]{:S(2)}) collective-permute-start(f32[1,2,1,512,256]{4,3,2,1,0:T(8,128)} %slice.46), channel_id=1, source_target_pairs={{0,6},{2,0},{4,2},{6,4},{1,7},{3,1},{5,3},{7,5},{8,14},{10,8},{12,... | collective-permute-start | bytes 3145736 | tf_op jit(solution)/shard_map/ppermute | solution.py:64
  151.9 1.7 copy-start.2
  153.6 22.6 %collective-permute-start.7 = (f32[1,2,1,512,256]{4,3,2,1,0:T(8,128)}, f32[1,2,1,512,256]{4,3,2,1,0:T(8,128)}, u32[]{:S(2)}, u32[]{:S(2)}) collective-permute-start(f32[1,2,1,512,256]{4,3,2,1,0:T(8,128)} %slice.47), channel_id=1, source_target_pairs={{0,2},{2,4},{4,6},{6,0},{1,3},{3,5},{5,7},{7,1},{8,10},{10,12},{12... | collective-permute-start | bytes 3145736 | tf_op jit(solution)/shard_map/ppermute | solution.py:65
  153.6 5.6 %copy-start.1 = (f32[1,4,1,512,256]{4,3,2,1,0:T(8,128)S(1)}, f32[1,4,1,512,256]{4,3,2,1,0:T(8,128)}, u32[]{:S(2)}) copy-start(f32[1,4,1,512,256]{4,3,2,1,0:T(8,128)} %copy-done) | copy-start | bytes 6291460
  153.6 7.1 %copy-start.3 = (f32[1,4,1,512,256]{4,3,2,1,0:T(8,128)S(1)}, f32[1,4,1,512,256]{4,3,2,1,0:T(8,128)}, u32[]{:S(2)}) copy-start(f32[1,4,1,512,256]{4,3,2,1,0:T(8,128)} %copy-done.2) | copy-start | bytes 6291460
  178.5 19.0 %slice-start = ((s8[8388608]{0:T(1024)(128)(4,1)}), s8[4194304]{0:T(1024)(128)(4,1)S(1)}, s32[]{:S(2)}) async-start(s8[8388608]{0:T(1024)(128)(4,1)} %bitcast.50), calls=%async_computation.5 | async-start | bytes 8388608
  188.4 9.1 %slice-start.1 = ((s8[8388608]{0:T(1024)(128)(4,1)}), s8[4194304]{0:T(1024)(128)(4,1)S(1)}, s32[]{:S(2)}) async-start(s8[8388608]{0:T(1024)(128)(4,1)} %bitcast.50), calls=%async_computation.6 | async-start | bytes 8388608
  204.5 9.0 %copy-start.5 = (f32[1,2,256,256]{3,2,1,0:T(8,128)S(1)}, f32[1,2,256,256]{3,2,1,0:T(8,128)}, u32[]{:S(2)}) copy-start(f32[1,2,256,256]{3,2,1,0:T(8,128)} %param.4) | copy-start | bytes 1572868
  213.6 11.1 %copy-start.4 = (f32[1,2,256,256]{3,2,1,0:T(8,128)}, f32[1,2,256,256]{3,2,1,0:T(8,128)S(1)}, u32[]{:S(2)}) copy-start(f32[1,2,256,256]{3,2,1,0:T(8,128)S(1)} %fusion.28) | copy-start | bytes 1572868
Sparse Core Ops, SparseCore 0:
  10.4 26.8 all-gather.5
  39.7 31.7 all-gather.7
  73.2 89.3 all-gather.9
  241.6 132.0 reduce-scatter.1

commit v4 on v3

--- a/solution.py
+++ b/solution.py
@@ -80,12 +80,26 @@
     return buf_ref[0]
 
 
+def pair_gather(block, axis_name, axis):
+    i = lax.axis_index(axis_name)
+    other = lax.ppermute(block, axis_name, [(0, 1), (1, 0)])
+    shape = list(block.shape)
+    blk = shape[axis]
+    shape[axis] = 2 * blk
+    starts = [0] * len(shape)
+    buf = jnp.zeros(shape, block.dtype)
+    starts[axis] = i * blk
+    buf = lax.dynamic_update_slice(buf, block, starts)
+    starts[axis] = (1 - i) * blk
+    return lax.dynamic_update_slice(buf, other, starts)
+
+
 def local(data, impulse, wavelet, live):
     positions = impulse.shape[3]
     total_shots = data.shape[3] * lax.axis_size(SHOT)
     scale = -(total_shots ** (-0.5))
     mask, observed, panel = make_panel(data, wavelet, live, total_shots, positions)
-    g = lax.all_gather(panel, "zl", axis=2, tiled=True)
+    g = pair_gather(panel, "zl", 2)
     g_re = lax.all_gather(g[:, 0], "y", axis=1, tiled=True)
     g_re = lax.all_gather(g_re, "x", axis=1, tiled=True)
     f, rows2, cols = g[:, 1].shape

time: 381 us -> 363 us (0.953)
  waiting for transfers between devices: 273 us -> 264 us
  matrix products: 62.7 us -> 55.4 us
    all_gather x1 -> x0, waiting for transfers between devices: 27 us -> none  [local(): g = lax.all_gather(panel, 'zl', axis=2, tiled=True)]
    ppermute x0 -> x1, waiting for transfers between devices: none -> 11.6 us  [pair_gather(): other = lax.ppermute(block, axis_name, [(0, 1), (1, 0)])]
    dot_general x6, matrix products: 62.7 us -> 55.4 us  [product(): jnp.einsum(form, left, right, precision=lax.Precision.HIGH, preferred_ele...]
    unnamed x16 -> x22, local copies, waits for them, and re-layouts: 0.6 us -> 5.59 us
    dynamic_update_slice x10, local copies, waits for them, and re-layouts: 9.12 us -> 4.17 us  [at(): return lax.dynamic_update_slice(buf_ref[0], part, starts)]
    ppermute x2, waiting for transfers between devices: 19.3 us -> 23.5 us  [ring_gather(): lax.ppermute(lax.slice_in_dim(right, 0, h, axis=split_axis), axis_name, bwd)]
where the time goes in v4:
time: 363 us
  waiting for transfers between devices  264 us (73%)
  matrix products  55.4 us (15%)
  local copies, waits for them, and re-layouts  15.2 us (4%)
  between operations  14.1 us (4%)
  starting transfers between devices  11.8 us (3%)
    reduce_scatter x1, waiting for transfers between devices, local(): gradient = lax.psum_scatter(terms, SHOT, scatter_dimension=3, tiled=True)  132 us
    dot_general x6, matrix products, product(): jnp.einsum(form, left, right, precision=lax.Precision.HIGH, preferred_ele...  55.4 us
    ppermute x2, waiting for transfers between devices, ring_gather(): right = lax.ppermute(block, axis_name, bwd)  54 us
    all_gather x1, waiting for transfers between devices, local(): g_re = lax.all_gather(g[:, 0], 'y', axis=1, tiled=True)  33.5 us
    ppermute x2, waiting for transfers between devices, ring_gather(): lax.ppermute(lax.slice_in_dim(right, 0, h, axis=split_axis), axis_name, bwd)  23.5 us
    ppermute x1, waiting for transfers between devices, pair_gather(): other = lax.ppermute(block, axis_name, [(0, 1), (1, 0)])  11.6 us
    ppermute x2, waiting for transfers between devices, ring_gather(): lax.ppermute(lax.slice_in_dim(left, h, 2 * h, axis=split_axis), axis_name...  9 us
  transfers between devices with their start and end apart: 12, of which 9 were waited for; matrix products, arithmetic and copies ran while one was open for 4% of the time, Pallas kernels for 0%

profile of v4, /device:TPU:1, one launch (start us, length us, event | category | flops | bytes accessed | tf_op | source)
XLA Modules:
  0.0 362.8 jit_solution(7054085378022013389)
XLA Ops:
  7.2 1.0 convert_element_type.10
  8.4 1.2 constant_dynamic-update-slice_fusion.11
  9.6 2.5 collective-permute-start
  12.1 11.6 %collective-permute-done = f32[1,2,256,256]{3,2,1,0:T(8,128)S(1)} collective-permute-done((f32[1,2,256,256]{3,2,1,0:T(8,128)S(1)}, f32[1,2,256,256]{3,2,1,0:T(8,128)S(1)}, u32[]{:S(2)}, u32[]{:S(2)}) %collective-permute-start) | collective-permute-done | bytes 524320 | tf_op jit(solution)/shard_map/ppermute | solution.py:85
  23.8 1.0 slice_bitcast_fusion
  24.9 33.5 %all-gather.5.cloned.1.call-done = f32[1,1,2048,256]{3,2,1,0:T(8,128)} async-done(((f32[1,1,512,256]{3,2,1,0:T(8,128)}), f32[1,1,2048,256]{3,2,1,0:T(8,128)}) %all-gather.5.cloned.1.call-update) | async-done | bytes 2097168 | tf_op jit(solution)/shard_map/all_gather | solution.py:103
  58.5 2.5 collective-permute-start.1
  61.0 10.8 %collective-permute-done.1 = f32[1,1,1,512,256]{4,3,2,1,0:T(8,128)S(1)} collective-permute-done((f32[1,1,1,512,256]{4,3,2,1,0:T(8,128)}, f32[1,1,1,512,256]{4,3,2,1,0:T(8,128)S(1)}, u32[]{:S(2)}, u32[]{:S(2)}) %collective-permute-start.1) | collective-permute-done | bytes 524320 | tf_op jit(solution)/shard_map/ppermute | solution.py:62
  71.8 0.8 copy-done.8
  72.5 3.3 collective-permute-start.3
  76.1 1.0 slice.45
  77.1 1.1 constant_dynamic-update-slice_fusion.8
  78.2 1.1 constant_dynamic-update-slice_fusion.7
  79.3 7.7 %collective-permute-done.3 = f32[1,1,1,256,256]{4,3,2,1,0:T(8,128)S(1)} collective-permute-done((f32[1,1,1,256,256]{4,3,2,1,0:T(8,128)S(1)}, f32[1,1,1,256,256]{4,3,2,1,0:T(8,128)S(1)}, u32[]{:S(2)}, u32[]{:S(2)}) %collective-permute-start.3) | collective-permute-done | bytes 262176 | tf_op jit(solution)/shard_map/ppermute | solution.py:64
  87.1 4.7 %collective-permute-done.4 = f32[1,1,1,256,256]{4,3,2,1,0:T(8,128)S(1)} collective-permute-done((f32[1,1,1,256,256]{4,3,2,1,0:T(8,128)S(1)}, f32[1,1,1,256,256]{4,3,2,1,0:T(8,128)S(1)}, u32[]{:S(2)}, u32[]{:S(2)}) %collective-permute-start.4) | collective-permute-done | bytes 262176 | tf_op jit(solution)/shard_map/ppermute | solution.py:65
  92.4 0.9 collective-permute-start.6
  93.3 43.2 %collective-permute-done.5 = f32[1,4,1,512,256]{4,3,2,1,0:T(8,128)S(1)} collective-permute-done((f32[1,4,1,512,256]{4,3,2,1,0:T(8,128)S(1)}, f32[1,4,1,512,256]{4,3,2,1,0:T(8,128)S(1)}, u32[]{:S(2)}, u32[]{:S(2)}) %collective-permute-start.5) | collective-permute-done | bytes 2097184 | tf_op jit(solution)/shard_map/ppermute | solution.py:62
  136.5 1.1 slice.46
  137.7 1.8 collective-permute-start.7
  139.5 1.2 slice.47
  141.2 0.8 broadcast_in_dim.14
  143.6 15.8 %collective-permute-done.7 = f32[1,2,1,512,256]{4,3,2,1,0:T(8,128)S(1)} collective-permute-done((f32[1,2,1,512,256]{4,3,2,1,0:T(8,128)}, f32[1,2,1,512,256]{4,3,2,1,0:T(8,128)S(1)}, u32[]{:S(2)}, u32[]{:S(2)}) %collective-permute-start.7) | collective-permute-done | bytes 1048608 | tf_op jit(solution)/shard_map/ppermute | solution.py:64
  159.4 4.3 %collective-permute-done.8 = f32[1,2,1,512,256]{4,3,2,1,0:T(8,128)} collective-permute-done((f32[1,2,1,512,256]{4,3,2,1,0:T(8,128)}, f32[1,2,1,512,256]{4,3,2,1,0:T(8,128)}, u32[]{:S(2)}, u32[]{:S(2)}) %collective-permute-start.8) | collective-permute-done | bytes 1048608 | tf_op jit(solution)/shard_map/ppermute | solution.py:65
  163.8 1.3 constant_dynamic-update-slice_fusion
  165.1 3.2 copy-done
  168.3 7.0 %fusion.2 = f32[256,256]{0,1:T(8,128)S(1)} fusion(f32[8192,256]{1,0:T(8,128)S(1)} %bitcast.53, f32[1,2,256,8192]{3,2,1,0:T(8,128)} %param.5), kind=kOutput, calls=%fused_computation.3 | convolution fusion | flops 3221225472 | bytes 17039360 | tf_op jit(solution)/shard_map/frk,fks->frs/dot_general | solution.py:11
  175.4 9.1 %fusion = f32[256,256]{0,1:T(8,128)S(1)} fusion(f32[1,1,8192,256]{3,2,1,0:T(8,128)} %all-gather.7.cloned.1.call-done, f32[1,2,256,8192]{3,2,1,0:T(8,128)} %param.5), kind=kOutput, calls=%fused_computation.1 | convolution fusion | flops 3221225472 | bytes 17039360 | tf_op jit(solution)/shard_map/frk,fks->frs/dot_general | solution.py:11
  184.5 7.2 %fusion.29 = f32[1,1,256,256]{3,2,1,0:T(8,128)S(1)} fusion(f32[256,256]{0,1:T(8,128)S(1)} %fusion, f32[8192,256]{1,0:T(8,128)S(1)} %bitcast.54, f32[1,2,256,8192]{3,2,1,0:T(8,128)} %param.5), kind=kOutput, calls=%fused_computation.20 | convolution fusion | flops 3221291008 | bytes 17301504 | tf_op jit(solution)/shard_map/frk,fks->frs/dot_general | solution.py:11
  191.7 7.1 %fusion.21 = f32[1,1,256,256]{3,2,1,0:T(8,128)S(1)} fusion(f32[256,256]{0,1:T(8,128)S(1)} %fusion.2, f32[1,2,256,8192]{3,2,1,0:T(8,128)} %param.5, f32[1,1,8192,256]{3,2,1,0:T(8,128)S(1)} %bitcast.58), kind=kOutput, calls=%fused_computation.18 | convolution fusion | flops 3221291008 | bytes 17301504 | tf_op jit(solution)/shard_map/frk,fks->frs/dot_general | solution.py:11
  199.0 11.0 %fusion.8 = f32[512,8192]{1,0:T(8,128)} fusion(f32[1,1,8192,256]{3,2,1,0:T(8,128)S(1)} %bitcast.58, f32[256,256]{1,0:T(8,128)S(1)} %get-tuple-element.7, f32[256,256]{1,0:T(8,128)S(1)} %get-tuple-element.6), kind=kOutput, calls=%fused_computation.9 | convolution fusion | flops 6442713088 | bytes 25690112 | tf_op jit(solution)/shard_map/frs,fks->frk/dot_general | solution.py:11
  209.9 14.1 %convolution_add_fusion = f32[512,8192]{1,0:T(8,128)} fusion(f32[512,8192]{1,0:T(8,128)} %fusion.8, f32[8192,256]{1,0:T(8,128)S(1)} %bitcast.55, f32[256,256]{1,0:T(8,128)S(1)} %fusion.43, f32[256,256]{1,0:T(8,128)S(1)} %get-tuple-element.7), kind=kOutput, calls=%fused_computation | convolution fusion | flops 6446907392 | bytes 42467328 | tf_op jit(solution)/shard_map/frs,fks->frk/dot_general | solution.py:11
  224.1 132.2 %reduce-scatter.2.cloned.1.call-done = f32[1,2,256,2048]{3,2,1,0:T(8,128)} async-done(((f32[1,2,256,8192]{3,2,1,0:T(8,128)}), f32[1,2,256,2048]{3,2,1,0:T(8,128)}) %reduce-scatter.2.cloned.1.call-update) | async-done | bytes 4194320 | tf_op jit(solution)/shard_map/reduce_scatter | solution.py:116
  (50 shorter events, 3.8 us)
Async XLA Ops:
  7.2 51.3 %all-gather.5.cloned.1.call-start = ((), (), s32[]{:S(2)}) async-start(), calls=%async_computation.2 | async-start | bytes 2621440 | tf_op jit(solution)/shard_map/all_gather | solution.py:103
  9.6 14.2 %collective-permute-start = (f32[1,2,256,256]{3,2,1,0:T(8,128)S(1)}, f32[1,2,256,256]{3,2,1,0:T(8,128)S(1)}, u32[]{:S(2)}, u32[]{:S(2)}) collective-permute-start(f32[1,2,256,256]{3,2,1,0:T(8,128)S(1)} %get-tuple-element.3), channel_id=1, source_target_pairs={{0,1},{1,0},{2,3},{3,2},{4,5},{5,4},{6,7},{7,6},{8,9},{9,8},{10,11... | collective-permute-start | bytes 1572872 | tf_op jit(solution)/shard_map/ppermute | solution.py:85
  24.9 150.5 %all-gather.7.cloned.1.call-start = ((), (), s32[]{:S(2)}) async-start(), calls=%async_computation.3 | async-start | bytes 10485760 | tf_op jit(solution)/shard_map/all_gather | solution.py:104
  58.5 297.8 %reduce-scatter.2.cloned.1.call-start = ((), (), s32[]{:S(2)}) async-start(), calls=%async_computation.1 | async-start | bytes 20971520 | tf_op jit(solution)/shard_map/reduce_scatter | solution.py:116
  58.5 13.2 %collective-permute-start.1 = (f32[1,1,1,512,256]{4,3,2,1,0:T(8,128)}, f32[1,1,1,512,256]{4,3,2,1,0:T(8,128)S(1)}, u32[]{:S(2)}, u32[]{:S(2)}) collective-permute-start(f32[1,1,1,512,256]{4,3,2,1,0:T(8,128)} %get-tuple-element.4), channel_id=1, source_target_pairs={{0,24},{8,0},{16,8},{24,16},{1,25},{9,1},{17,9},{25,17},{2,26},{10... | collective-permute-start | bytes 1572872 | tf_op jit(solution)/shard_map/ppermute | solution.py:62
  61.0 15.1 %collective-permute-start.2 = (f32[1,1,1,512,256]{4,3,2,1,0:T(8,128)}, f32[1,1,1,512,256]{4,3,2,1,0:T(8,128)}, u32[]{:S(2)}, u32[]{:S(2)}) collective-permute-start(f32[1,1,1,512,256]{4,3,2,1,0:T(8,128)} %get-tuple-element.4), channel_id=1, source_target_pairs={{0,8},{8,16},{16,24},{24,0},{1,9},{9,17},{17,25},{25,1},{2,10},{10... | collective-permute-start | bytes 1572872 | tf_op jit(solution)/shard_map/ppermute | solution.py:61
  71.7 0.8 copy-start.8
  72.5 14.5 %collective-permute-start.3 = (f32[1,1,1,256,256]{4,3,2,1,0:T(8,128)S(1)}, f32[1,1,1,256,256]{4,3,2,1,0:T(8,128)S(1)}, u32[]{:S(2)}, u32[]{:S(2)}) collective-permute-start(f32[1,1,1,256,256]{4,3,2,1,0:T(8,128)S(1)} %slice.44), channel_id=1, source_target_pairs={{0,24},{8,0},{16,8},{24,16},{1,25},{9,1},{17,9},{25,17},{2,26},{10... | collective-permute-start | bytes 786440 | tf_op jit(solution)/shard_map/ppermute | solution.py:64
  77.0 14.7 %collective-permute-start.4 = (f32[1,1,1,256,256]{4,3,2,1,0:T(8,128)S(1)}, f32[1,1,1,256,256]{4,3,2,1,0:T(8,128)S(1)}, u32[]{:S(2)}, u32[]{:S(2)}) collective-permute-start(f32[1,1,1,256,256]{4,3,2,1,0:T(8,128)S(1)} %slice.45), channel_id=1, source_target_pairs={{0,8},{8,16},{16,24},{24,0},{1,9},{9,17},{17,25},{25,1},{2,10},{10... | collective-permute-start | bytes 786440 | tf_op jit(solution)/shard_map/ppermute | solution.py:65
  91.7 44.8 %collective-permute-start.5 = (f32[1,4,1,512,256]{4,3,2,1,0:T(8,128)S(1)}, f32[1,4,1,512,256]{4,3,2,1,0:T(8,128)S(1)}, u32[]{:S(2)}, u32[]{:S(2)}) collective-permute-start(f32[1,4,1,512,256]{4,3,2,1,0:T(8,128)S(1)} %constant_dynamic-update-slice_fusion.5), channel_id=1, source_target_pairs={{0,6},{2,0},{4,2},{6,4},{1,7},{3,1},{5,3},{7,5},{8,14},{10,8},{12,... | collective-permute-start | bytes 6291464 | tf_op jit(solution)/shard_map/ppermute | solution.py:62
  92.4 47.1 %collective-permute-start.6 = (f32[1,4,1,512,256]{4,3,2,1,0:T(8,128)S(1)}, f32[1,4,1,512,256]{4,3,2,1,0:T(8,128)S(1)}, u32[]{:S(2)}, u32[]{:S(2)}) collective-permute-start(f32[1,4,1,512,256]{4,3,2,1,0:T(8,128)S(1)} %constant_dynamic-update-slice_fusion.5), channel_id=1, source_target_pairs={{0,2},{2,4},{4,6},{6,0},{1,3},{3,5},{5,7},{7,1},{8,10},{10,12},{12... | collective-permute-start | bytes 6291464 | tf_op jit(solution)/shard_map/ppermute | solution.py:61
  136.5 2.9 copy-start.2
  137.7 21.7 %collective-permute-start.7 = (f32[1,2,1,512,256]{4,3,2,1,0:T(8,128)}, f32[1,2,1,512,256]{4,3,2,1,0:T(8,128)S(1)}, u32[]{:S(2)}, u32[]{:S(2)}) collective-permute-start(f32[1,2,1,512,256]{4,3,2,1,0:T(8,128)} %slice.46), channel_id=1, source_target_pairs={{0,6},{2,0},{4,2},{6,4},{1,7},{3,1},{5,3},{7,5},{8,14},{10,8},{12,... | collective-permute-start | bytes 3145736 | tf_op jit(solution)/shard_map/ppermute | solution.py:64
  139.5 1.7 copy-start.4
  141.2 22.6 %collective-permute-start.8 = (f32[1,2,1,512,256]{4,3,2,1,0:T(8,128)}, f32[1,2,1,512,256]{4,3,2,1,0:T(8,128)}, u32[]{:S(2)}, u32[]{:S(2)}) collective-permute-start(f32[1,2,1,512,256]{4,3,2,1,0:T(8,128)} %slice.47), channel_id=1, source_target_pairs={{0,2},{2,4},{4,6},{6,0},{1,3},{3,5},{5,7},{7,1},{8,10},{10,12},{12... | collective-permute-start | bytes 3145736 | tf_op jit(solution)/shard_map/ppermute | solution.py:65
  141.2 1.6 copy-start.3
  141.2 2.2 copy-start.5
  165.1 3.2 copy-start
  175.4 9.1 %copy-start.1 = (f32[1,4,4,512,256]{4,3,2,1,0:T(8,128)S(1)}, f32[1,4,4,512,256]{4,3,2,1,0:T(8,128)}, u32[]{:S(2)}) copy-start(f32[1,4,4,512,256]{4,3,2,1,0:T(8,128)} %copy-done) | copy-start | bytes 25165828
  175.4 16.3 %slice-start = ((s8[8388608]{0:T(1024)(128)(4,1)}), s8[4194304]{0:T(1024)(128)(4,1)S(1)}, s32[]{:S(2)}) async-start(s8[8388608]{0:T(1024)(128)(4,1)} %bitcast.57), calls=%async_computation.4 | async-start | bytes 8388608
  184.5 7.2 %slice-start.1 = ((s8[8388608]{0:T(1024)(128)(4,1)}), s8[4194304]{0:T(1024)(128)(4,1)S(1)}, s32[]{:S(2)}) async-start(s8[8388608]{0:T(1024)(128)(4,1)} %bitcast.57), calls=%async_computation.5 | async-start | bytes 8388608
  191.7 7.1 %copy-start.7 = (f32[1,2,256,256]{3,2,1,0:T(8,128)S(1)}, f32[1,2,256,256]{3,2,1,0:T(8,128)}, u32[]{:S(2)}) copy-start(f32[1,2,256,256]{3,2,1,0:T(8,128)} %param.4) | copy-start | bytes 1572868
  198.9 11.0 %copy-start.6 = (f32[1,2,256,256]{3,2,1,0:T(8,128)}, f32[1,2,256,256]{3,2,1,0:T(8,128)S(1)}, u32[]{:S(2)}) copy-start(f32[1,2,256,256]{3,2,1,0:T(8,128)S(1)} %fusion.32) | copy-start | bytes 1572868
Sparse Core Ops, SparseCore 0:
  25.0 33.3 all-gather.4
  60.1 89.3 all-gather.6
  224.2 132.0 reduce-scatter.1

commit v5 on v4

--- a/solution.py
+++ b/solution.py
@@ -101,7 +101,8 @@
     mask, observed, panel = make_panel(data, wavelet, live, total_shots, positions)
     g = pair_gather(panel, "zl", 2)
     g_re = lax.all_gather(g[:, 0], "y", axis=1, tiled=True)
-    g_re = lax.all_gather(g_re, "x", axis=1, tiled=True)
+    f0, rows8, cols0 = g_re.shape
+    g_re = ring_gather(g_re.reshape(f0, 1, rows8, cols0), "x", 1, 2).reshape(f0, 4 * rows8, cols0)
     f, rows2, cols = g[:, 1].shape
     gx = ring_gather(g[:, 1].reshape(f, 1, 1, rows2, cols), "x", 1, 3)
     gy = ring_gather(gx, "y", 2, 1)

time: 363 us -> 347 us (0.956)
  waiting for transfers between devices: 264 us -> 230 us
  starting transfers between devices: 11.8 us -> 21.7 us
  local copies, waits for them, and re-layouts: 15.2 us -> 24.3 us
    all_gather x1, waiting for transfers between devices: 33.5 us -> 8.1 us  [local(): g_re = lax.all_gather(g[:, 0], 'y', axis=1, tiled=True)]
    ppermute x2 -> x3, waiting for transfers between devices: 54 us -> 45.3 us  [ring_gather(): right = lax.ppermute(block, axis_name, bwd)]
    dynamic_update_slice x10 -> x15, local copies, waits for them, and re-layouts: 4.17 us -> 12.6 us  [at(): return lax.dynamic_update_slice(buf_ref[0], part, starts)]
    ppermute x2 -> x3, starting transfers between devices: 3.13 us -> 10.9 us  [ring_gather(): right = lax.ppermute(block, axis_name, bwd)]
    unnamed x22 -> x8, local copies, waits for them, and re-layouts: 5.59 us -> 0.79 us
    ppermute x2 -> x3, waiting for transfers between devices: 9 us -> 11.7 us  [ring_gather(): lax.ppermute(lax.slice_in_dim(left, h, 2 * h, axis=split_axis), axis_name...]
    ppermute x2 -> x3, starting transfers between devices: 5.1 us -> 7.42 us  [ring_gather(): lax.ppermute(lax.slice_in_dim(right, 0, h, axis=split_axis), axis_name, bwd)]
    ppermute x2 -> x3, waiting for transfers between devices: 23.5 us -> 22 us  [ring_gather(): lax.ppermute(lax.slice_in_dim(right, 0, h, axis=split_axis), axis_name, bwd)]
  transfers between devices with their start and end apart: 12 -> 15, of which waited for: 9 -> 10; matrix products, arithmetic and copies ran while one was open for 4% -> 8% of each run, Pallas kernels for 0% -> 0%
where the time goes in v5:
time: 347 us; the launch traced here: 346 us
  waiting for transfers between devices  230 us (66%)
  matrix products  53.1 us (15%)
  local copies, waits for them, and re-layouts  24.3 us (7%)
  starting transfers between devices  21.7 us (6%)
  between operations  14.4 us (4%)
    reduce_scatter x1, waiting for transfers between devices, local(): gradient = lax.psum_scatter(terms, SHOT, scatter_dimension=3, tiled=True)  131 us
    dot_general x6, matrix products, product(): jnp.einsum(form, left, right, precision=lax.Precision.HIGH, preferred_ele...  53.1 us
    ppermute x3, waiting for transfers between devices, ring_gather(): right = lax.ppermute(block, axis_name, bwd)  45.3 us
    ppermute x3, waiting for transfers between devices, ring_gather(): lax.ppermute(lax.slice_in_dim(right, 0, h, axis=split_axis), axis_name, bwd)  22 us
    dynamic_update_slice x15, local copies, waits for them, and re-layouts, at(): return lax.dynamic_update_slice(buf_ref[0], part, starts)  12.6 us
    ppermute x3, waiting for transfers between devices, ring_gather(): lax.ppermute(lax.slice_in_dim(left, h, 2 * h, axis=split_axis), axis_name...  11.7 us
    ppermute x1, waiting for transfers between devices, pair_gather(): other = lax.ppermute(block, axis_name, [(0, 1), (1, 0)])  11.6 us
    ppermute x3, starting transfers between devices, ring_gather(): right = lax.ppermute(block, axis_name, bwd)  10.9 us
  transfers between devices with their start and end apart: 15, of which 10 were waited for; matrix products, arithmetic and copies ran while one was open for 8% of the time, Pallas kernels for 0%

profile of v5, /device:TPU:1, one launch (start us, length us, event | category | flops | bytes accessed | tf_op | source)
XLA Modules:
  0.0 346.1 jit_solution(15417606622196383965)
XLA Ops:
  9.6 2.5 collective-permute-start
  12.1 11.6 %collective-permute-done = f32[1,2,256,256]{3,2,1,0:T(8,128)S(1)} collective-permute-done((f32[1,2,256,256]{3,2,1,0:T(8,128)S(1)}, f32[1,2,256,256]{3,2,1,0:T(8,128)S(1)}, u32[]{:S(2)}, u32[]{:S(2)}) %collective-permute-start) | collective-permute-done | bytes 524320 | tf_op jit(solution)/shard_map/ppermute | solution.py:85
  24.9 2.4 collective-permute-start.5
  27.4 10.2 %collective-permute-done.5 = f32[1,1,1,512,256]{4,3,2,1,0:T(8,128)S(1)} collective-permute-done((f32[1,1,1,512,256]{4,3,2,1,0:T(8,128)}, f32[1,1,1,512,256]{4,3,2,1,0:T(8,128)S(1)}, u32[]{:S(2)}, u32[]{:S(2)}) %collective-permute-start.5) | collective-permute-done | bytes 524320 | tf_op jit(solution)/shard_map/ppermute | solution.py:62
  38.4 3.3 collective-permute-start.7
  45.2 4.6 %collective-permute-done.8 = f32[1,1,1,256,256]{4,3,2,1,0:T(8,128)S(1)} collective-permute-done((f32[1,1,1,256,256]{4,3,2,1,0:T(8,128)S(1)}, f32[1,1,1,256,256]{4,3,2,1,0:T(8,128)S(1)}, u32[]{:S(2)}, u32[]{:S(2)}) %collective-permute-start.8) | collective-permute-done | bytes 262176 | tf_op jit(solution)/shard_map/ppermute | solution.py:65
  49.8 2.8 collective-permute-start.9
  52.7 8.1 %all-gather.3.cloned.1.call-done = f32[1,1,2048,256]{3,2,1,0:T(8,128)} async-done(((f32[1,1,512,256]{3,2,1,0:T(8,128)}), f32[1,1,2048,256]{3,2,1,0:T(8,128)}) %all-gather.3.cloned.1.call-update) | async-done | bytes 2097168 | tf_op jit(solution)/shard_map/all_gather | solution.py:103
  60.8 5.6 %collective-permute-start.1 = (f32[1,1,2048,256]{3,2,1,0:T(8,128)}, f32[1,1,2048,256]{3,2,1,0:T(8,128)}, u32[]{:S(2)}, u32[]{:S(2)}) collective-permute-start(f32[1,1,2048,256]{3,2,1,0:T(8,128)} %all-gather.3.cloned.1.call-done), channel_id=1, source_target_pairs={{0,24},{8,0},{16,8},{24,16},{1,25},{9,1},{17,9},{25,17},{2,26},{10... | collective-permute-start | bytes 6291464 | tf_op jit(solution)/shard_map/ppermute | solution.py:62
  66.4 35.0 %collective-permute-done.9 = f32[1,4,1,512,256]{4,3,2,1,0:T(8,128)} collective-permute-done((f32[1,4,1,512,256]{4,3,2,1,0:T(8,128)S(1)}, f32[1,4,1,512,256]{4,3,2,1,0:T(8,128)}, u32[]{:S(2)}, u32[]{:S(2)}) %collective-permute-start.9) | collective-permute-done | bytes 2097184 | tf_op jit(solution)/shard_map/ppermute | solution.py:62
  101.4 2.3 slice.56
  104.7 2.3 slice.57
  108.5 1.9 constant_dynamic-update-slice_fusion.3
  110.4 1.8 constant_dynamic-update-slice_fusion.2
  113.0 14.1 %collective-permute-done.11 = f32[1,2,1,512,256]{4,3,2,1,0:T(8,128)} collective-permute-done((f32[1,2,1,512,256]{4,3,2,1,0:T(8,128)}, f32[1,2,1,512,256]{4,3,2,1,0:T(8,128)}, u32[]{:S(2)}, u32[]{:S(2)}) %collective-permute-start.11) | collective-permute-done | bytes 1048608 | tf_op jit(solution)/shard_map/ppermute | solution.py:64
  127.1 1.3 constant_dynamic-update-slice_fusion.1
  128.4 2.7 collective-permute-done.12
  131.2 1.3 constant_dynamic-update-slice_fusion
  132.5 1.3 slice.51
  133.8 3.1 collective-permute-start.3
  136.9 1.3 slice.52
  138.4 7.0 %fusion.2 = f32[256,256]{0,1:T(8,128)S(1)} fusion(f32[8192,256]{1,0:T(8,128)S(1)} %bitcast.46, f32[1,2,256,8192]{3,2,1,0:T(8,128)} %param.5), kind=kOutput, calls=%fused_computation.3 | convolution fusion | flops 3221225472 | bytes 17039360 | tf_op jit(solution)/shard_map/frk,fks->frs/dot_general | solution.py:11
  145.4 1.8 constant_dynamic-update-slice_fusion.13
  147.2 1.8 constant_dynamic-update-slice_fusion.12
  149.0 7.8 %collective-permute-done.3 = f32[1,1,1024,256]{3,2,1,0:T(8,128)S(1)} collective-permute-done((f32[1,1,1024,256]{3,2,1,0:T(8,128)S(1)}, f32[1,1,1024,256]{3,2,1,0:T(8,128)S(1)}, u32[]{:S(2)}, u32[]{:S(2)}) %collective-permute-start.3) | collective-permute-done | bytes 1048608 | tf_op jit(solution)/shard_map/ppermute | solution.py:64
  156.9 4.4 %collective-permute-done.4 = f32[1,1,1024,256]{3,2,1,0:T(8,128)S(1)} collective-permute-done((f32[1,1,1024,256]{3,2,1,0:T(8,128)S(1)}, f32[1,1,1024,256]{3,2,1,0:T(8,128)S(1)}, u32[]{:S(2)}, u32[]{:S(2)}) %collective-permute-start.4) | collective-permute-done | bytes 1048608 | tf_op jit(solution)/shard_map/ppermute | solution.py:65
  161.4 7.0 %fusion = f32[256,256]{0,1:T(8,128)S(1)} fusion(f32[8192,256]{1,0:T(8,128)S(1)} %bitcast.49, f32[1,2,256,8192]{3,2,1,0:T(8,128)} %param.5), kind=kOutput, calls=%fused_computation.1 | convolution fusion | flops 3221225472 | bytes 17039360 | tf_op jit(solution)/shard_map/frk,fks->frs/dot_general | solution.py:11
  168.4 7.0 %fusion.15 = f32[1,1,256,256]{3,2,1,0:T(8,128)S(1)} fusion(f32[256,256]{0,1:T(8,128)S(1)} %fusion.2, f32[8192,256]{1,0:T(8,128)S(1)} %bitcast.50, f32[1,2,256,8192]{3,2,1,0:T(8,128)} %param.5), kind=kOutput, calls=%fused_computation.14 | convolution fusion | flops 3221291008 | bytes 17301504 | tf_op jit(solution)/shard_map/frk,fks->frs/dot_general | solution.py:11
  175.4 7.1 %fusion.21 = f32[1,1,256,256]{3,2,1,0:T(8,128)S(1)} fusion(f32[256,256]{0,1:T(8,128)S(1)} %fusion, f32[8192,256]{1,0:T(8,128)S(1)} %bitcast.47, f32[1,2,256,8192]{3,2,1,0:T(8,128)} %param.5), kind=kOutput, calls=%fused_computation.16 | convolution fusion | flops 3221291008 | bytes 17301504 | tf_op jit(solution)/shard_map/frk,fks->frs/dot_general | solution.py:11
  182.7 10.9 %fusion.27 = f32[512,8192]{1,0:T(8,128)} fusion(f32[8192,256]{1,0:T(8,128)S(1)} %bitcast.48, f32[256,256]{1,0:T(8,128)S(1)} %fusion.36, f32[256,256]{1,0:T(8,128)S(1)} %get-tuple-element.7), kind=kOutput, calls=%fused_computation.24 | convolution fusion | flops 6442713088 | bytes 25690112 | tf_op jit(solution)/shard_map/frs,fks->frk/dot_general | solution.py:11
  193.6 14.1 %convolution_add_fusion = f32[512,8192]{1,0:T(8,128)} fusion(f32[512,8192]{1,0:T(8,128)} %fusion.27, f32[8192,256]{1,0:T(8,128)S(1)} %bitcast.51, f32[256,256]{1,0:T(8,128)S(1)} %get-tuple-element.7, f32[256,256]{1,0:T(8,128)S(1)} %get-tuple-element.6), kind=kOutput, calls=%fused_computation | convolution fusion | flops 6446907392 | bytes 42467328 | tf_op jit(solution)/shard_map/frs,fks->frk/dot_general | solution.py:11
  207.7 131.5 %reduce-scatter.2.cloned.1.call-done = f32[1,2,256,2048]{3,2,1,0:T(8,128)} async-done(((f32[1,2,256,8192]{3,2,1,0:T(8,128)}), f32[1,2,256,2048]{3,2,1,0:T(8,128)}) %reduce-scatter.2.cloned.1.call-update) | async-done | bytes 4194320 | tf_op jit(solution)/shard_map/reduce_scatter | solution.py:117
  (48 shorter events, 11.6 us)
Async XLA Ops:
  7.2 53.6 %all-gather.3.cloned.1.call-start = ((), (), s32[]{:S(2)}) async-start(), calls=%async_computation.2 | async-start | bytes 2621440 | tf_op jit(solution)/shard_map/all_gather | solution.py:103
  9.6 14.2 %collective-permute-start = (f32[1,2,256,256]{3,2,1,0:T(8,128)S(1)}, f32[1,2,256,256]{3,2,1,0:T(8,128)S(1)}, u32[]{:S(2)}, u32[]{:S(2)}) collective-permute-start(f32[1,2,256,256]{3,2,1,0:T(8,128)S(1)} %get-tuple-element.3), channel_id=1, source_target_pairs={{0,1},{1,0},{2,3},{3,2},{4,5},{5,4},{6,7},{7,6},{8,9},{9,8},{10,11... | collective-permute-start | bytes 1572872 | tf_op jit(solution)/shard_map/ppermute | solution.py:85
  24.9 314.3 %reduce-scatter.2.cloned.1.call-start = ((), (), s32[]{:S(2)}) async-start(), calls=%async_computation.1 | async-start | bytes 20971520 | tf_op jit(solution)/shard_map/reduce_scatter | solution.py:117
  24.9 12.7 %collective-permute-start.5 = (f32[1,1,1,512,256]{4,3,2,1,0:T(8,128)}, f32[1,1,1,512,256]{4,3,2,1,0:T(8,128)S(1)}, u32[]{:S(2)}, u32[]{:S(2)}) collective-permute-start(f32[1,1,1,512,256]{4,3,2,1,0:T(8,128)} %get-tuple-element.4), channel_id=1, source_target_pairs={{0,24},{8,0},{16,8},{24,16},{1,25},{9,1},{17,9},{25,17},{2,26},{10... | collective-permute-start | bytes 1572872 | tf_op jit(solution)/shard_map/ppermute | solution.py:62
  27.4 14.6 %collective-permute-start.6 = (f32[1,1,1,512,256]{4,3,2,1,0:T(8,128)}, f32[1,1,1,512,256]{4,3,2,1,0:T(8,128)}, u32[]{:S(2)}, u32[]{:S(2)}) collective-permute-start(f32[1,1,1,512,256]{4,3,2,1,0:T(8,128)} %get-tuple-element.4), channel_id=1, source_target_pairs={{0,8},{8,16},{16,24},{24,0},{1,9},{9,17},{17,25},{25,1},{2,10},{10... | collective-permute-start | bytes 1572872 | tf_op jit(solution)/shard_map/ppermute | solution.py:61
  37.6 0.8 copy-start.3
  38.4 6.8 %collective-permute-start.7 = (f32[1,1,1,256,256]{4,3,2,1,0:T(8,128)S(1)}, f32[1,1,1,256,256]{4,3,2,1,0:T(8,128)S(1)}, u32[]{:S(2)}, u32[]{:S(2)}) collective-permute-start(f32[1,1,1,256,256]{4,3,2,1,0:T(8,128)S(1)} %slice.54), channel_id=1, source_target_pairs={{0,24},{8,0},{16,8},{24,16},{1,25},{9,1},{17,9},{25,17},{2,26},{10... | collective-permute-start | bytes 786440 | tf_op jit(solution)/shard_map/ppermute | solution.py:64
  42.9 6.9 %collective-permute-start.8 = (f32[1,1,1,256,256]{4,3,2,1,0:T(8,128)S(1)}, f32[1,1,1,256,256]{4,3,2,1,0:T(8,128)S(1)}, u32[]{:S(2)}, u32[]{:S(2)}) collective-permute-start(f32[1,1,1,256,256]{4,3,2,1,0:T(8,128)S(1)} %slice.55), channel_id=1, source_target_pairs={{0,8},{8,16},{16,24},{24,0},{1,9},{9,17},{17,25},{25,1},{2,10},{10... | collective-permute-start | bytes 786440 | tf_op jit(solution)/shard_map/ppermute | solution.py:65
  49.8 51.6 %collective-permute-start.9 = (f32[1,4,1,512,256]{4,3,2,1,0:T(8,128)S(1)}, f32[1,4,1,512,256]{4,3,2,1,0:T(8,128)}, u32[]{:S(2)}, u32[]{:S(2)}) collective-permute-start(f32[1,4,1,512,256]{4,3,2,1,0:T(8,128)S(1)} %constant_dynamic-update-slice_fusion.5), channel_id=1, source_target_pairs={{0,6},{2,0},{4,2},{6,4},{1,7},{3,1},{5,3},{7,5},{8,14},{10,8},{12,... | collective-permute-start | bytes 6291464 | tf_op jit(solution)/shard_map/ppermute | solution.py:62
  52.6 52.1 %collective-permute-start.10 = (f32[1,4,1,512,256]{4,3,2,1,0:T(8,128)S(1)}, f32[1,4,1,512,256]{4,3,2,1,0:T(8,128)}, u32[]{:S(2)}, u32[]{:S(2)}) collective-permute-start(f32[1,4,1,512,256]{4,3,2,1,0:T(8,128)S(1)} %constant_dynamic-update-slice_fusion.5), channel_id=1, source_target_pairs={{0,2},{2,4},{4,6},{6,0},{1,3},{3,5},{5,7},{7,1},{8,10},{10,12},{12... | collective-permute-start | bytes 6291464 | tf_op jit(solution)/shard_map/ppermute | solution.py:61
  60.8 71.7 %collective-permute-start.1 = (f32[1,1,2048,256]{3,2,1,0:T(8,128)}, f32[1,1,2048,256]{3,2,1,0:T(8,128)}, u32[]{:S(2)}, u32[]{:S(2)}) collective-permute-start(f32[1,1,2048,256]{3,2,1,0:T(8,128)} %all-gather.3.cloned.1.call-done), channel_id=1, source_target_pairs={{0,24},{8,0},{16,8},{24,16},{1,25},{9,1},{17,9},{25,17},{2,26},{10... | collective-permute-start | bytes 6291464 | tf_op jit(solution)/shard_map/ppermute | solution.py:62
  66.4 70.5 %collective-permute-start.2 = (f32[1,1,2048,256]{3,2,1,0:T(8,128)}, f32[1,1,2048,256]{3,2,1,0:T(8,128)}, u32[]{:S(2)}, u32[]{:S(2)}) collective-permute-start(f32[1,1,2048,256]{3,2,1,0:T(8,128)} %all-gather.3.cloned.1.call-done), channel_id=1, source_target_pairs={{0,8},{8,16},{16,24},{24,0},{1,9},{9,17},{17,25},{25,1},{2,10},{10... | collective-permute-start | bytes 6291464 | tf_op jit(solution)/shard_map/ppermute | solution.py:61
  103.7 23.4 %collective-permute-start.11 = (f32[1,2,1,512,256]{4,3,2,1,0:T(8,128)}, f32[1,2,1,512,256]{4,3,2,1,0:T(8,128)}, u32[]{:S(2)}, u32[]{:S(2)}) collective-permute-start(f32[1,2,1,512,256]{4,3,2,1,0:T(8,128)} %slice.56), channel_id=1, source_target_pairs={{0,6},{2,0},{4,2},{6,4},{1,7},{3,1},{5,3},{7,5},{8,14},{10,8},{12,... | collective-permute-start | bytes 3145736 | tf_op jit(solution)/shard_map/ppermute | solution.py:64
  107.0 24.1 %collective-permute-start.12 = (f32[1,2,1,512,256]{4,3,2,1,0:T(8,128)}, f32[1,2,1,512,256]{4,3,2,1,0:T(8,128)}, u32[]{:S(2)}, u32[]{:S(2)}) collective-permute-start(f32[1,2,1,512,256]{4,3,2,1,0:T(8,128)} %slice.57), channel_id=1, source_target_pairs={{0,2},{2,4},{4,6},{6,0},{1,3},{3,5},{5,7},{7,1},{8,10},{10,12},{12... | collective-permute-start | bytes 3145736 | tf_op jit(solution)/shard_map/ppermute | solution.py:65
  108.5 4.4 %copy-start.1 = (f32[1,1,2048,256]{3,2,1,0:T(8,128)S(1)}, f32[1,1,2048,256]{3,2,1,0:T(8,128)}, u32[]{:S(2)}) copy-start(f32[1,1,2048,256]{3,2,1,0:T(8,128)} %all-gather.3.cloned.1.call-done) | copy-start | bytes 6291460
  133.8 23.0 %collective-permute-start.3 = (f32[1,1,1024,256]{3,2,1,0:T(8,128)S(1)}, f32[1,1,1024,256]{3,2,1,0:T(8,128)S(1)}, u32[]{:S(2)}, u32[]{:S(2)}) collective-permute-start(f32[1,1,1024,256]{3,2,1,0:T(8,128)S(1)} %slice.51), channel_id=1, source_target_pairs={{0,24},{8,0},{16,8},{24,16},{1,25},{9,1},{17,9},{25,17},{2,26},{10... | collective-permute-start | bytes 3145736 | tf_op jit(solution)/shard_map/ppermute | solution.py:64
  138.2 23.1 %collective-permute-start.4 = (f32[1,1,1024,256]{3,2,1,0:T(8,128)S(1)}, f32[1,1,1024,256]{3,2,1,0:T(8,128)S(1)}, u32[]{:S(2)}, u32[]{:S(2)}) collective-permute-start(f32[1,1,1024,256]{3,2,1,0:T(8,128)S(1)} %slice.52), channel_id=1, source_target_pairs={{0,8},{8,16},{16,24},{24,0},{1,9},{9,17},{17,25},{25,1},{2,10},{10... | collective-permute-start | bytes 3145736 | tf_op jit(solution)/shard_map/ppermute | solution.py:65
  175.4 7.1 %copy-start.2 = (f32[1,2,256,256]{3,2,1,0:T(8,128)S(1)}, f32[1,2,256,256]{3,2,1,0:T(8,128)}, u32[]{:S(2)}) copy-start(f32[1,2,256,256]{3,2,1,0:T(8,128)} %param.4) | copy-start | bytes 1572868
  182.6 11.0 %copy-start = (f32[1,2,256,256]{3,2,1,0:T(8,128)}, f32[1,2,256,256]{3,2,1,0:T(8,128)S(1)}, u32[]{:S(2)}) copy-start(f32[1,2,256,256]{3,2,1,0:T(8,128)S(1)} %fusion.24) | copy-start | bytes 1572868
Sparse Core Ops, SparseCore 0:
  25.0 35.7 all-gather.2
  207.8 131.3 reduce-scatter.1

commit v6 on v5

--- a/solution.py
+++ b/solution.py
@@ -53,31 +53,36 @@
     return Mesh(devs, ("zh", "c", "x", "y", "zl"))
 
 
-def ring_gather(block, axis_name, axis, split_axis):
+def ring_near(block, axis_name):
+    n = lax.axis_size(axis_name)
+    fwd = [(s, (s + 1) % n) for s in range(n)]
+    bwd = [(s, (s - 1) % n) for s in range(n)]
+    return lax.ppermute(block, axis_name, fwd), lax.ppermute(block, axis_name, bwd)
+
+
+def ring_far(block, left, right, axis_name, axis, split_axis):
     n = lax.axis_size(axis_name)
     i = lax.axis_index(axis_name)
     fwd = [(s, (s + 1) % n) for s in range(n)]
     bwd = [(s, (s - 1) % n) for s in range(n)]
-    left = lax.ppermute(block, axis_name, fwd)
-    right = lax.ppermute(block, axis_name, bwd)
     h = block.shape[split_axis] // 2
     far_a = lax.ppermute(lax.slice_in_dim(right, 0, h, axis=split_axis), axis_name, bwd)
     far_b = lax.ppermute(lax.slice_in_dim(left, h, 2 * h, axis=split_axis), axis_name, fwd)
     shape = list(block.shape)
     shape[axis] = n
     buf = jnp.zeros(shape, block.dtype)
-
-    def at(part, slot, offset):
+    for part, slot, offset in ((block, i, 0), (right, (i + 1) % n, 0), (left, (i + n - 1) % n, 0),
+                               (far_a, (i + 2) % n, 0), (far_b, (i + 2) % n, h)):
         starts = [0] * len(shape)
         starts[axis] = slot
         starts[split_axis] = offset
-        return lax.dynamic_update_slice(buf_ref[0], part, starts)
+        buf = lax.dynamic_update_slice(buf, part, starts)
+    return buf
 
-    buf_ref = [buf]
-    for part, slot, offset in ((block, i, 0), (right, (i + 1) % n, 0), (left, (i + n - 1) % n, 0),
-                               (far_a, (i + 2) % n, 0), (far_b, (i + 2) % n, h)):
-        buf_ref[0] = at(part, slot, offset)
-    return buf_ref[0]
+
+def ring_gather(block, axis_name, axis, split_axis):
+    left, right = ring_near(block, axis_name)
+    return ring_far(block, left, right, axis_name, axis, split_axis)
 
 
 def pair_gather(block, axis_name, axis):
@@ -102,11 +107,14 @@
     g = pair_gather(panel, "zl", 2)
     g_re = lax.all_gather(g[:, 0], "y", axis=1, tiled=True)
     f0, rows8, cols0 = g_re.shape
-    g_re = ring_gather(g_re.reshape(f0, 1, rows8, cols0), "x", 1, 2).reshape(f0, 4 * rows8, cols0)
     f, rows2, cols = g[:, 1].shape
     gx = ring_gather(g[:, 1].reshape(f, 1, 1, rows2, cols), "x", 1, 3)
-    gy = ring_gather(gx, "y", 2, 1)
-    g_im = gy.reshape(f, 16 * rows2, cols)
+    b_re = g_re.reshape(f0, 1, rows8, cols0)
+    l_re, r_re = ring_near(b_re, "x")
+    l_im, r_im = ring_near(gx, "y")
+    l_re, r_re, l_im, r_im = lax.optimization_barrier((l_re, r_re, l_im, r_im))
+    g_re = ring_far(b_re, l_re, r_re, "x", 1, 2).reshape(f0, 4 * rows8, cols0)
+    g_im = ring_far(gx, l_im, r_im, "y", 2, 1).reshape(f, 16 * rows2, cols)
     g = jnp.stack([g_re, g_im], axis=1)
     predicted = convolve(impulse, g)
     residual = mask[None, None] * (observed - predicted)

time: 347 us -> 339 us (0.977)
  local copies, waits for them, and re-layouts: 24.3 us -> 19.7 us
    ppermute x12, waiting for transfers between devices: 79 us -> 72.1 us  [the longest x3 45.3 us: ring_near(): lax.ppermute(block, axis_name, bwd)]
  transfers between devices with their start and end apart: 15 -> 15, of which waited for: 10 -> 12; matrix products, arithmetic and copies ran while one was open for 8% -> 7% of each run, Pallas kernels for 0% -> 0%
where the time goes in v6:
time: 339 us
  waiting for transfers between devices  227 us (67%)
  matrix products  53.1 us (16%)
  starting transfers between devices  22.4 us (7%)
  local copies, waits for them, and re-layouts  19.7 us (6%)
  between operations  14.4 us (4%)
    reduce_scatter x1, waiting for transfers between devices, local(): gradient = lax.psum_scatter(terms, SHOT, scatter_dimension=3, tiled=True)  135 us
    dot_general x6, matrix products, product(): jnp.einsum(form, left, right, precision=lax.Precision.HIGH, preferred_ele...  53.1 us
    ppermute x3, waiting for transfers between devices, ring_near(): lax.ppermute(block, axis_name, bwd)  45.3 us
    ppermute x3, waiting for transfers between devices, ring_far(): lax.ppermute(lax.slice_in_dim(right, 0, h, axis=split_axis), axis_name, bwd)  12.1 us
    ppermute x1, waiting for transfers between devices, pair_gather(): other = lax.ppermute(block, axis_name, [(0, 1), (1, 0)])  11.6 us
    dynamic_update_slice x15, local copies, waits for them, and re-layouts, ring_far(): buf = lax.dynamic_update_slice(buf, part, starts)  10 us
    ppermute x3, waiting for transfers between devices, ring_near(): lax.ppermute(block, axis_name, fwd)  9.75 us
    all_gather x1, waiting for transfers between devices, local(): g_re = lax.all_gather(g[:, 0], 'y', axis=1, tiled=True)  8.1 us
  transfers between devices with their start and end apart: 15, of which 12 were waited for; matrix products, arithmetic and copies ran while one was open for 7% of the time, Pallas kernels for 0%

profile of v6, /device:TPU:1, one launch (start us, length us, event | category | flops | bytes accessed | tf_op | source)
XLA Modules:
  0.0 338.5 jit_solution(13909841651529946166)
XLA Ops:
  9.6 2.5 collective-permute-start
  12.1 11.6 %collective-permute-done = f32[1,2,256,256]{3,2,1,0:T(8,128)S(1)} collective-permute-done((f32[1,2,256,256]{3,2,1,0:T(8,128)S(1)}, f32[1,2,256,256]{3,2,1,0:T(8,128)S(1)}, u32[]{:S(2)}, u32[]{:S(2)}) %collective-permute-start) | collective-permute-done | bytes 524320 | tf_op jit(solution)/shard_map/ppermute | solution.py:90
  24.9 2.4 collective-permute-start.3
  27.4 10.2 %collective-permute-done.3 = f32[1,1,1,512,256]{4,3,2,1,0:T(8,128)S(1)} collective-permute-done((f32[1,1,1,512,256]{4,3,2,1,0:T(8,128)}, f32[1,1,1,512,256]{4,3,2,1,0:T(8,128)S(1)}, u32[]{:S(2)}, u32[]{:S(2)}) %collective-permute-start.3) | collective-permute-done | bytes 524320 | tf_op jit(solution)/shard_map/ppermute | solution.py:60
  38.4 3.3 collective-permute-start.5
  45.2 4.6 %collective-permute-done.6 = f32[1,1,1,256,256]{4,3,2,1,0:T(8,128)S(1)} collective-permute-done((f32[1,1,1,256,256]{4,3,2,1,0:T(8,128)S(1)}, f32[1,1,1,256,256]{4,3,2,1,0:T(8,128)S(1)}, u32[]{:S(2)}, u32[]{:S(2)}) %collective-permute-start.6) | collective-permute-done | bytes 262176 | tf_op jit(solution)/shard_map/ppermute | solution.py:70
  49.8 2.8 collective-permute-start.8
  52.7 8.1 %all-gather.3.cloned.1.call-done = f32[1,1,2048,256]{3,2,1,0:T(8,128)} async-done(((f32[1,1,512,256]{3,2,1,0:T(8,128)}), f32[1,1,2048,256]{3,2,1,0:T(8,128)}) %all-gather.3.cloned.1.call-update) | async-done | bytes 2097168 | tf_op jit(solution)/shard_map/all_gather | solution.py:108
  60.8 3.5 %collective-permute-start.1 = (f32[1,1,2048,256]{3,2,1,0:T(8,128)}, f32[1,1,2048,256]{3,2,1,0:T(8,128)}, u32[]{:S(2)}, u32[]{:S(2)}) collective-permute-start(f32[1,1,2048,256]{3,2,1,0:T(8,128)} %all-gather.3.cloned.1.call-done), channel_id=1, source_target_pairs={{0,8},{8,16},{16,24},{24,0},{1,9},{9,17},{17,25},{25,1},{2,10},{10... | collective-permute-start | bytes 6291464 | tf_op jit(solution)/shard_map/ppermute | solution.py:60
  64.3 2.1 collective-permute-start.2
  67.4 34.0 %collective-permute-done.8 = f32[1,4,1,512,256]{4,3,2,1,0:T(8,128)} collective-permute-done((f32[1,4,1,512,256]{4,3,2,1,0:T(8,128)S(1)}, f32[1,4,1,512,256]{4,3,2,1,0:T(8,128)}, u32[]{:S(2)}, u32[]{:S(2)}) %collective-permute-start.8) | collective-permute-done | bytes 2097184 | tf_op jit(solution)/shard_map/ppermute | solution.py:60
  101.5 9.6 %collective-permute-done.1 = f32[1,1,2048,256]{3,2,1,0:T(8,128)} collective-permute-done((f32[1,1,2048,256]{3,2,1,0:T(8,128)}, f32[1,1,2048,256]{3,2,1,0:T(8,128)}, u32[]{:S(2)}, u32[]{:S(2)}) %collective-permute-start.1) | collective-permute-done | bytes 2097184 | tf_op jit(solution)/shard_map/ppermute | solution.py:60
  112.2 1.3 slice.45
  113.5 1.3 slice.46
  116.0 1.6 collective-permute-start.11
  118.4 1.3 slice.42
  119.7 1.3 slice.43
  121.0 1.2 collective-permute-start.10
  122.2 1.5 collective-permute-start.9
  123.8 1.8 constant_dynamic-update-slice_fusion.3
  125.5 1.8 constant_dynamic-update-slice_fusion.2
  127.3 1.8 constant_dynamic-update-slice_fusion.8
  129.1 1.8 constant_dynamic-update-slice_fusion.7
  130.8 7.2 %collective-permute-done.11 = f32[1,2,1,512,256]{4,3,2,1,0:T(8,128)S(1)} collective-permute-done((f32[1,2,1,512,256]{4,3,2,1,0:T(8,128)S(1)}, f32[1,2,1,512,256]{4,3,2,1,0:T(8,128)S(1)}, u32[]{:S(2)}, u32[]{:S(2)}) %collective-permute-start.11) | collective-permute-done | bytes 1048608 | tf_op jit(solution)/shard_map/ppermute | solution.py:69
  138.6 4.9 %collective-permute-done.9 = f32[1,1,1024,256]{3,2,1,0:T(8,128)S(1)} collective-permute-done((f32[1,1,1024,256]{3,2,1,0:T(8,128)S(1)}, f32[1,1,1024,256]{3,2,1,0:T(8,128)S(1)}, u32[]{:S(2)}, u32[]{:S(2)}) %collective-permute-start.9) | collective-permute-done | bytes 1048608 | tf_op jit(solution)/shard_map/ppermute | solution.py:69
  143.5 7.0 %fusion.2 = f32[256,256]{0,1:T(8,128)S(1)} fusion(f32[8192,256]{1,0:T(8,128)S(1)} %bitcast.49, f32[1,2,256,8192]{3,2,1,0:T(8,128)} %param.5), kind=kOutput, calls=%fused_computation.3 | convolution fusion | flops 3221225472 | bytes 17039360 | tf_op jit(solution)/shard_map/frk,fks->frs/dot_general | solution.py:11
  150.6 7.0 %fusion = f32[256,256]{0,1:T(8,128)S(1)} fusion(f32[8192,256]{1,0:T(8,128)S(1)} %bitcast.46, f32[1,2,256,8192]{3,2,1,0:T(8,128)} %param.5), kind=kOutput, calls=%fused_computation.1 | convolution fusion | flops 3221225472 | bytes 17039360 | tf_op jit(solution)/shard_map/frk,fks->frs/dot_general | solution.py:11
  157.7 7.0 %fusion.15 = f32[1,1,256,256]{3,2,1,0:T(8,128)S(1)} fusion(f32[256,256]{0,1:T(8,128)S(1)} %fusion.2, f32[8192,256]{1,0:T(8,128)S(1)} %bitcast.47, f32[1,2,256,8192]{3,2,1,0:T(8,128)} %param.5), kind=kOutput, calls=%fused_computation.14 | convolution fusion | flops 3221291008 | bytes 17301504 | tf_op jit(solution)/shard_map/frk,fks->frs/dot_general | solution.py:11
  164.7 7.1 %fusion.21 = f32[1,1,256,256]{3,2,1,0:T(8,128)S(1)} fusion(f32[256,256]{0,1:T(8,128)S(1)} %fusion, f32[8192,256]{1,0:T(8,128)S(1)} %bitcast.50, f32[1,2,256,8192]{3,2,1,0:T(8,128)} %param.5), kind=kOutput, calls=%fused_computation.16 | convolution fusion | flops 3221291008 | bytes 17301504 | tf_op jit(solution)/shard_map/frk,fks->frs/dot_general | solution.py:11
  172.0 10.9 %fusion.27 = f32[512,8192]{1,0:T(8,128)} fusion(f32[8192,256]{1,0:T(8,128)S(1)} %bitcast.51, f32[256,256]{1,0:T(8,128)S(1)} %fusion.36, f32[256,256]{1,0:T(8,128)S(1)} %get-tuple-element.15), kind=kOutput, calls=%fused_computation.24 | convolution fusion | flops 6442713088 | bytes 25690112 | tf_op jit(solution)/shard_map/frs,fks->frk/dot_general | solution.py:11
  182.9 14.1 %convolution_add_fusion = f32[512,8192]{1,0:T(8,128)} fusion(f32[512,8192]{1,0:T(8,128)} %fusion.27, f32[8192,256]{1,0:T(8,128)S(1)} %bitcast.48, f32[256,256]{1,0:T(8,128)S(1)} %get-tuple-element.15, f32[256,256]{1,0:T(8,128)S(1)} %get-tuple-element.14), kind=kOutput, calls=%fused_computation | convolution fusion | flops 6446907392 | bytes 42467328 | tf_op jit(solution)/shard_map/frs,fks->frk/dot_general | solution.py:11
  197.0 134.7 %reduce-scatter.2.cloned.1.call-done = f32[1,2,256,2048]{3,2,1,0:T(8,128)} async-done(((f32[1,2,256,8192]{3,2,1,0:T(8,128)}), f32[1,2,256,2048]{3,2,1,0:T(8,128)}) %reduce-scatter.2.cloned.1.call-update) | async-done | bytes 4194320 | tf_op jit(solution)/shard_map/reduce_scatter | solution.py:125
  (48 shorter events, 12.7 us)
Async XLA Ops:
  7.2 53.6 %all-gather.3.cloned.1.call-start = ((), (), s32[]{:S(2)}) async-start(), calls=%async_computation.2 | async-start | bytes 2621440 | tf_op jit(solution)/shard_map/all_gather | solution.py:108
  9.6 14.2 %collective-permute-start = (f32[1,2,256,256]{3,2,1,0:T(8,128)S(1)}, f32[1,2,256,256]{3,2,1,0:T(8,128)S(1)}, u32[]{:S(2)}, u32[]{:S(2)}) collective-permute-start(f32[1,2,256,256]{3,2,1,0:T(8,128)S(1)} %get-tuple-element.11), channel_id=1, source_target_pairs={{0,1},{1,0},{2,3},{3,2},{4,5},{5,4},{6,7},{7,6},{8,9},{9,8},{10,11... | collective-permute-start | bytes 1572872 | tf_op jit(solution)/shard_map/ppermute | solution.py:90
  24.9 306.8 %reduce-scatter.2.cloned.1.call-start = ((), (), s32[]{:S(2)}) async-start(), calls=%async_computation.1 | async-start | bytes 20971520 | tf_op jit(solution)/shard_map/reduce_scatter | solution.py:125
  24.9 12.7 %collective-permute-start.3 = (f32[1,1,1,512,256]{4,3,2,1,0:T(8,128)}, f32[1,1,1,512,256]{4,3,2,1,0:T(8,128)S(1)}, u32[]{:S(2)}, u32[]{:S(2)}) collective-permute-start(f32[1,1,1,512,256]{4,3,2,1,0:T(8,128)} %get-tuple-element.12), channel_id=1, source_target_pairs={{0,24},{8,0},{16,8},{24,16},{1,25},{9,1},{17,9},{25,17},{2,26},{10... | collective-permute-start | bytes 1572872 | tf_op jit(solution)/shard_map/ppermute | solution.py:60
  27.4 14.6 %collective-permute-start.4 = (f32[1,1,1,512,256]{4,3,2,1,0:T(8,128)}, f32[1,1,1,512,256]{4,3,2,1,0:T(8,128)}, u32[]{:S(2)}, u32[]{:S(2)}) collective-permute-start(f32[1,1,1,512,256]{4,3,2,1,0:T(8,128)} %get-tuple-element.12), channel_id=1, source_target_pairs={{0,8},{8,16},{16,24},{24,0},{1,9},{9,17},{17,25},{25,1},{2,10},{10... | collective-permute-start | bytes 1572872 | tf_op jit(solution)/shard_map/ppermute | solution.py:60
  37.6 0.8 copy-start.3
  38.4 6.8 %collective-permute-start.5 = (f32[1,1,1,256,256]{4,3,2,1,0:T(8,128)S(1)}, f32[1,1,1,256,256]{4,3,2,1,0:T(8,128)S(1)}, u32[]{:S(2)}, u32[]{:S(2)}) collective-permute-start(f32[1,1,1,256,256]{4,3,2,1,0:T(8,128)S(1)} %slice.52), channel_id=1, source_target_pairs={{0,24},{8,0},{16,8},{24,16},{1,25},{9,1},{17,9},{25,17},{2,26},{10... | collective-permute-start | bytes 786440 | tf_op jit(solution)/shard_map/ppermute | solution.py:69
  42.9 6.9 %collective-permute-start.6 = (f32[1,1,1,256,256]{4,3,2,1,0:T(8,128)S(1)}, f32[1,1,1,256,256]{4,3,2,1,0:T(8,128)S(1)}, u32[]{:S(2)}, u32[]{:S(2)}) collective-permute-start(f32[1,1,1,256,256]{4,3,2,1,0:T(8,128)S(1)} %slice.53), channel_id=1, source_target_pairs={{0,8},{8,16},{16,24},{24,0},{1,9},{9,17},{17,25},{25,1},{2,10},{10... | collective-permute-start | bytes 786440 | tf_op jit(solution)/shard_map/ppermute | solution.py:70
  49.8 51.6 %collective-permute-start.8 = (f32[1,4,1,512,256]{4,3,2,1,0:T(8,128)S(1)}, f32[1,4,1,512,256]{4,3,2,1,0:T(8,128)}, u32[]{:S(2)}, u32[]{:S(2)}) collective-permute-start(f32[1,4,1,512,256]{4,3,2,1,0:T(8,128)S(1)} %constant_dynamic-update-slice_fusion.9), channel_id=1, source_target_pairs={{0,6},{2,0},{4,2},{6,4},{1,7},{3,1},{5,3},{7,5},{8,14},{10,8},{12,... | collective-permute-start | bytes 6291464 | tf_op jit(solution)/shard_map/ppermute | solution.py:60
  52.6 48.9 %collective-permute-start.7 = (f32[1,4,1,512,256]{4,3,2,1,0:T(8,128)S(1)}, f32[1,4,1,512,256]{4,3,2,1,0:T(8,128)}, u32[]{:S(2)}, u32[]{:S(2)}) collective-permute-start(f32[1,4,1,512,256]{4,3,2,1,0:T(8,128)S(1)} %constant_dynamic-update-slice_fusion.9), channel_id=1, source_target_pairs={{0,2},{2,4},{4,6},{6,0},{1,3},{3,5},{5,7},{7,1},{8,10},{10,12},{12... | collective-permute-start | bytes 6291464 | tf_op jit(solution)/shard_map/ppermute | solution.py:60
  60.8 50.4 %collective-permute-start.1 = (f32[1,1,2048,256]{3,2,1,0:T(8,128)}, f32[1,1,2048,256]{3,2,1,0:T(8,128)}, u32[]{:S(2)}, u32[]{:S(2)}) collective-permute-start(f32[1,1,2048,256]{3,2,1,0:T(8,128)} %all-gather.3.cloned.1.call-done), channel_id=1, source_target_pairs={{0,8},{8,16},{16,24},{24,0},{1,9},{9,17},{17,25},{25,1},{2,10},{10... | collective-permute-start | bytes 6291464 | tf_op jit(solution)/shard_map/ppermute | solution.py:60
  64.3 47.9 %collective-permute-start.2 = (f32[1,1,2048,256]{3,2,1,0:T(8,128)}, f32[1,1,2048,256]{3,2,1,0:T(8,128)}, u32[]{:S(2)}, u32[]{:S(2)}) collective-permute-start(f32[1,1,2048,256]{3,2,1,0:T(8,128)} %all-gather.3.cloned.1.call-done), channel_id=1, source_target_pairs={{0,24},{8,0},{16,8},{24,16},{1,25},{9,1},{17,9},{25,17},{2,26},{10... | collective-permute-start | bytes 6291464 | tf_op jit(solution)/shard_map/ppermute | solution.py:60
  67.2 51.0 %copy-start.1 = (f32[1,1,2048,256]{3,2,1,0:T(8,128)S(1)}, f32[1,1,2048,256]{3,2,1,0:T(8,128)}, u32[]{:S(2)}) copy-start(f32[1,1,2048,256]{3,2,1,0:T(8,128)} %all-gather.3.cloned.1.call-done) | copy-start | bytes 6291460
  114.8 23.6 %collective-permute-start.12 = (f32[1,2,1,512,256]{4,3,2,1,0:T(8,128)S(1)}, f32[1,2,1,512,256]{4,3,2,1,0:T(8,128)S(1)}, u32[]{:S(2)}, u32[]{:S(2)}) collective-permute-start(f32[1,2,1,512,256]{4,3,2,1,0:T(8,128)S(1)} %slice.46), channel_id=1, source_target_pairs={{0,2},{2,4},{4,6},{6,0},{1,3},{3,5},{5,7},{7,1},{8,10},{10,12},{12... | collective-permute-start | bytes 3145736 | tf_op jit(solution)/shard_map/ppermute | solution.py:70
  116.0 22.1 %collective-permute-start.11 = (f32[1,2,1,512,256]{4,3,2,1,0:T(8,128)S(1)}, f32[1,2,1,512,256]{4,3,2,1,0:T(8,128)S(1)}, u32[]{:S(2)}, u32[]{:S(2)}) collective-permute-start(f32[1,2,1,512,256]{4,3,2,1,0:T(8,128)S(1)} %slice.45), channel_id=1, source_target_pairs={{0,6},{2,0},{4,2},{6,4},{1,7},{3,1},{5,3},{7,5},{8,14},{10,8},{12,... | collective-permute-start | bytes 3145736 | tf_op jit(solution)/shard_map/ppermute | solution.py:69
  121.0 29.5 %collective-permute-start.10 = (f32[1,1,1024,256]{3,2,1,0:T(8,128)S(1)}, f32[1,1,1024,256]{3,2,1,0:T(8,128)S(1)}, u32[]{:S(2)}, u32[]{:S(2)}) collective-permute-start(f32[1,1,1024,256]{3,2,1,0:T(8,128)S(1)} %slice.43), channel_id=1, source_target_pairs={{0,8},{8,16},{16,24},{24,0},{1,9},{9,17},{17,25},{25,1},{2,10},{10... | collective-permute-start | bytes 3145736 | tf_op jit(solution)/shard_map/ppermute | solution.py:70
  122.2 21.2 %collective-permute-start.9 = (f32[1,1,1024,256]{3,2,1,0:T(8,128)S(1)}, f32[1,1,1024,256]{3,2,1,0:T(8,128)S(1)}, u32[]{:S(2)}, u32[]{:S(2)}) collective-permute-start(f32[1,1,1024,256]{3,2,1,0:T(8,128)S(1)} %slice.42), channel_id=1, source_target_pairs={{0,24},{8,0},{16,8},{24,16},{1,25},{9,1},{17,9},{25,17},{2,26},{10... | collective-permute-start | bytes 3145736 | tf_op jit(solution)/shard_map/ppermute | solution.py:69
  164.7 7.1 %copy-start.2 = (f32[1,2,256,256]{3,2,1,0:T(8,128)S(1)}, f32[1,2,256,256]{3,2,1,0:T(8,128)}, u32[]{:S(2)}) copy-start(f32[1,2,256,256]{3,2,1,0:T(8,128)} %param.4) | copy-start | bytes 1572868
  171.9 11.0 %copy-start = (f32[1,2,256,256]{3,2,1,0:T(8,128)}, f32[1,2,256,256]{3,2,1,0:T(8,128)S(1)}, u32[]{:S(2)}) copy-start(f32[1,2,256,256]{3,2,1,0:T(8,128)S(1)} %fusion.24) | copy-start | bytes 1572868
Sparse Core Ops, SparseCore 0:
  25.0 35.7 all-gather.2
  197.1 134.5 reduce-scatter.1

commit v7 on v6

--- a/solution.py
+++ b/solution.py
@@ -104,17 +104,18 @@
     total_shots = data.shape[3] * lax.axis_size(SHOT)
     scale = -(total_shots ** (-0.5))
     mask, observed, panel = make_panel(data, wavelet, live, total_shots, positions)
-    g = pair_gather(panel, "zl", 2)
-    g_re = lax.all_gather(g[:, 0], "y", axis=1, tiled=True)
+    g_re = pair_gather(panel[:, 0], "zl", 1)
+    g_re = lax.all_gather(g_re, "y", axis=1, tiled=True)
     f0, rows8, cols0 = g_re.shape
-    f, rows2, cols = g[:, 1].shape
-    gx = ring_gather(g[:, 1].reshape(f, 1, 1, rows2, cols), "x", 1, 3)
+    f, rows1, cols = panel[:, 1].shape
+    gx = ring_gather(panel[:, 1].reshape(f, 1, 1, 1, rows1, cols), "x", 1, 4)
+    gx = pair_gather(gx, "zl", 3)
     b_re = g_re.reshape(f0, 1, rows8, cols0)
     l_re, r_re = ring_near(b_re, "x")
     l_im, r_im = ring_near(gx, "y")
     l_re, r_re, l_im, r_im = lax.optimization_barrier((l_re, r_re, l_im, r_im))
     g_re = ring_far(b_re, l_re, r_re, "x", 1, 2).reshape(f0, 4 * rows8, cols0)
-    g_im = ring_far(gx, l_im, r_im, "y", 2, 1).reshape(f, 16 * rows2, cols)
+    g_im = ring_far(gx, l_im, r_im, "y", 2, 1).reshape(f, 32 * rows1, cols)
     g = jnp.stack([g_re, g_im], axis=1)
     predicted = convolve(impulse, g)
     residual = mask[None, None] * (observed - predicted)

time: 339 us -> 332 us (0.979)
  waiting for transfers between devices: 227 us -> 223 us
    ppermute x1 -> x2, waiting for transfers between devices: 11.6 us -> 25.7 us  [pair_gather(): other = lax.ppermute(block, axis_name, [(0, 1), (1, 0)])]
    all_gather x1, waiting for transfers between devices: 8.1 us -> 0.01 us  [local(): g_re = lax.all_gather(g_re, 'y', axis=1, tiled=True)]
    ppermute x3, waiting for transfers between devices: 9.75 us -> 3.45 us  [ring_near(): lax.ppermute(block, axis_name, fwd)]
    ppermute x3, waiting for transfers between devices: 45.3 us -> 41.3 us  [ring_near(): lax.ppermute(block, axis_name, bwd)]
    reduce_scatter x1, waiting for transfers between devices: 135 us -> 139 us  [local(): gradient = lax.psum_scatter(terms, SHOT, scatter_dimension=3, tiled=True)]
    ppermute x3, starting transfers between devices: 3.55 us -> 0.01 us  [ring_near(): lax.ppermute(block, axis_name, fwd)]
  transfers between devices with their start and end apart: 15 -> 16, of which waited for: 12 -> 12; matrix products, arithmetic and copies ran while one was open for 7% -> 6% of each run, Pallas kernels for 0% -> 0%
where the time goes in v7:
time: 332 us
  waiting for transfers between devices  223 us (67%)
  matrix products  53.1 us (16%)
  starting transfers between devices  21.6 us (7%)
  local copies, waits for them, and re-layouts  17.3 us (5%)
  between operations  14.4 us (4%)
    reduce_scatter x1, waiting for transfers between devices, local(): gradient = lax.psum_scatter(terms, SHOT, scatter_dimension=3, tiled=True)  139 us
    dot_general x6, matrix products, product(): jnp.einsum(form, left, right, precision=lax.Precision.HIGH, preferred_ele...  53.1 us
    ppermute x3, waiting for transfers between devices, ring_near(): lax.ppermute(block, axis_name, bwd)  41.3 us
    ppermute x2, waiting for transfers between devices, pair_gather(): other = lax.ppermute(block, axis_name, [(0, 1), (1, 0)])  25.7 us
    ppermute x3, waiting for transfers between devices, ring_far(): lax.ppermute(lax.slice_in_dim(right, 0, h, axis=split_axis), axis_name, bwd)  10.1 us
    ppermute x3, starting transfers between devices, ring_far(): lax.ppermute(lax.slice_in_dim(right, 0, h, axis=split_axis), axis_name, bwd)  8.81 us
    ppermute x3, starting transfers between devices, ring_near(): lax.ppermute(block, axis_name, bwd)  8.72 us
    dynamic_update_slice x15, local copies, waits for them, and re-layouts, ring_far(): buf = lax.dynamic_update_slice(buf, part, starts)  7.85 us
  transfers between devices with their start and end apart: 16, of which 12 were waited for; matrix products, arithmetic and copies ran while one was open for 6% of the time, Pallas kernels for 0%

profile of v7, /device:TPU:1, one launch (start us, length us, event | category | flops | bytes accessed | tf_op | source)
XLA Modules:
  0.0 331.9 jit_solution(11142053739204456953)
XLA Ops:
  9.5 2.5 collective-permute-start
  12.1 5.9 %collective-permute-done = f32[1,256,256]{2,1,0:T(8,128)S(1)} collective-permute-done((f32[1,256,256]{2,1,0:T(8,128)S(1)}, f32[1,256,256]{2,1,0:T(8,128)S(1)}, u32[]{:S(2)}, u32[]{:S(2)}) %collective-permute-start) | collective-permute-done | bytes 262176 | tf_op jit(solution)/shard_map/ppermute | solution.py:90
  19.0 2.4 collective-permute-start.3
  21.5 4.2 %collective-permute-done.3 = f32[1,1,1,1,256,256]{5,4,3,2,1,0:T(8,128)S(1)} collective-permute-done((f32[1,1,1,1,256,256]{5,4,3,2,1,0:T(8,128)S(1)}, f32[1,1,1,1,256,256]{5,4,3,2,1,0:T(8,128)S(1)}, u32[]{:S(2)}, u32[]{:S(2)}) %collective-permute-start.3) | collective-permute-done | bytes 262176 | tf_op jit(solution)/shard_map/ppermute | solution.py:60
  25.7 3.5 %collective-permute-start.5 = (f32[1,1,1,1,128,256]{5,4,3,2,1,0:T(8,128)S(1)}, f32[1,1,1,1,128,256]{5,4,3,2,1,0:T(8,128)S(1)}, u32[]{:S(2)}, u32[]{:S(2)}) collective-permute-start(f32[1,1,1,1,128,256]{5,4,3,2,1,0:T(8,128)S(1)} %slice.52), channel_id=1, source_target_pairs={{0,24},{8,0},{16,8},{24,16},{1,25},{9,1},{17,9},{25,17},{2,26},{10... | collective-permute-start | bytes 393224 | tf_op jit(solution)/shard_map/ppermute | solution.py:69
  29.4 1.8 collective-permute-done.5
  31.2 3.2 collective-permute-done.6
  35.8 19.8 %collective-permute-done.7 = f32[1,4,1,1,256,256]{5,4,3,2,1,0:T(8,128)} collective-permute-done((f32[1,4,1,1,256,256]{5,4,3,2,1,0:T(8,128)S(1)}, f32[1,4,1,1,256,256]{5,4,3,2,1,0:T(8,128)}, u32[]{:S(2)}, u32[]{:S(2)}) %collective-permute-start.7) | collective-permute-done | bytes 1048608 | tf_op jit(solution)/shard_map/ppermute | solution.py:90
  55.6 1.3 constant_dynamic-update-slice_fusion.9
  56.9 3.6 %collective-permute-start.9 = (f32[1,4,1,2,256,256]{5,4,3,2,1,0:T(8,128)S(1)}, f32[1,4,1,2,256,256]{5,4,3,2,1,0:T(8,128)}, u32[]{:S(2)}, u32[]{:S(2)}) collective-permute-start(f32[1,4,1,2,256,256]{5,4,3,2,1,0:T(8,128)S(1)} %constant_dynamic-update-slice_fusion.9), channel_id=1, source_target_pairs={{0,6},{2,0},{4,2},{6,4},{1,7},{3,1},{5,3},{7,5},{8,14},{10,8},{12,... | collective-permute-start | bytes 6291464 | tf_op jit(solution)/shard_map/ppermute | solution.py:60
  60.6 2.7 collective-permute-start.2
  64.4 37.1 %collective-permute-done.9 = f32[1,4,1,2,256,256]{5,4,3,2,1,0:T(8,128)} collective-permute-done((f32[1,4,1,2,256,256]{5,4,3,2,1,0:T(8,128)S(1)}, f32[1,4,1,2,256,256]{5,4,3,2,1,0:T(8,128)}, u32[]{:S(2)}, u32[]{:S(2)}) %collective-permute-start.9) | collective-permute-done | bytes 2097184 | tf_op jit(solution)/shard_map/ppermute | solution.py:60
  101.4 3.2 collective-permute-done.8
  104.9 1.3 slice.45
  106.2 1.3 slice.46
  107.6 2.7 collective-permute-start.12
  111.1 1.3 slice.42
  112.4 1.3 slice.43
  113.8 2.7 collective-permute-start.10
  116.4 1.8 constant_dynamic-update-slice_fusion.3
  118.2 1.8 constant_dynamic-update-slice_fusion.2
  120.0 1.8 constant_dynamic-update-slice_fusion.8
  121.8 1.8 constant_dynamic-update-slice_fusion.7
  123.5 3.7 %collective-permute-done.12 = f32[1,2,1,2,256,256]{5,4,3,2,1,0:T(8,128)S(1)} collective-permute-done((f32[1,2,1,2,256,256]{5,4,3,2,1,0:T(8,128)S(1)}, f32[1,2,1,2,256,256]{5,4,3,2,1,0:T(8,128)S(1)}, u32[]{:S(2)}, u32[]{:S(2)}) %collective-permute-start.12) | collective-permute-done | bytes 1048608 | tf_op jit(solution)/shard_map/ppermute | solution.py:69
  128.4 4.6 %collective-permute-done.10 = f32[1,1,1024,256]{3,2,1,0:T(8,128)S(1)} collective-permute-done((f32[1,1,1024,256]{3,2,1,0:T(8,128)S(1)}, f32[1,1,1024,256]{3,2,1,0:T(8,128)S(1)}, u32[]{:S(2)}, u32[]{:S(2)}) %collective-permute-start.10) | collective-permute-done | bytes 1048608 | tf_op jit(solution)/shard_map/ppermute | solution.py:69
  133.0 7.0 %fusion.2 = f32[256,256]{0,1:T(8,128)S(1)} fusion(f32[8192,256]{1,0:T(8,128)S(1)} %bitcast.55, f32[1,2,256,8192]{3,2,1,0:T(8,128)} %param.5), kind=kOutput, calls=%fused_computation.3 | convolution fusion | flops 3221225472 | bytes 17039360 | tf_op jit(solution)/shard_map/frk,fks->frs/dot_general | solution.py:11
  140.1 7.0 %fusion = f32[256,256]{0,1:T(8,128)S(1)} fusion(f32[8192,256]{1,0:T(8,128)S(1)} %bitcast.52, f32[1,2,256,8192]{3,2,1,0:T(8,128)} %param.5), kind=kOutput, calls=%fused_computation.1 | convolution fusion | flops 3221225472 | bytes 17039360 | tf_op jit(solution)/shard_map/frk,fks->frs/dot_general | solution.py:11
  147.2 7.0 %fusion.15 = f32[1,1,256,256]{3,2,1,0:T(8,128)S(1)} fusion(f32[256,256]{0,1:T(8,128)S(1)} %fusion.2, f32[8192,256]{1,0:T(8,128)S(1)} %bitcast.53, f32[1,2,256,8192]{3,2,1,0:T(8,128)} %param.5), kind=kOutput, calls=%fused_computation.14 | convolution fusion | flops 3221291008 | bytes 17301504 | tf_op jit(solution)/shard_map/frk,fks->frs/dot_general | solution.py:11
  154.2 7.1 %fusion.21 = f32[1,1,256,256]{3,2,1,0:T(8,128)S(1)} fusion(f32[256,256]{0,1:T(8,128)S(1)} %fusion, f32[8192,256]{1,0:T(8,128)S(1)} %bitcast.56, f32[1,2,256,8192]{3,2,1,0:T(8,128)} %param.5), kind=kOutput, calls=%fused_computation.16 | convolution fusion | flops 3221291008 | bytes 17301504 | tf_op jit(solution)/shard_map/frk,fks->frs/dot_general | solution.py:11
  161.5 10.9 %fusion.27 = f32[512,8192]{1,0:T(8,128)} fusion(f32[8192,256]{1,0:T(8,128)S(1)} %bitcast.57, f32[256,256]{1,0:T(8,128)S(1)} %fusion.36, f32[256,256]{1,0:T(8,128)S(1)} %get-tuple-element.11), kind=kOutput, calls=%fused_computation.23 | convolution fusion | flops 6442713088 | bytes 25690112 | tf_op jit(solution)/shard_map/frs,fks->frk/dot_general | solution.py:11
  172.4 14.1 %convolution_add_fusion = f32[512,8192]{1,0:T(8,128)} fusion(f32[512,8192]{1,0:T(8,128)} %fusion.27, f32[8192,256]{1,0:T(8,128)S(1)} %bitcast.54, f32[256,256]{1,0:T(8,128)S(1)} %get-tuple-element.11, f32[256,256]{1,0:T(8,128)S(1)} %get-tuple-element.10), kind=kOutput, calls=%fused_computation | convolution fusion | flops 6446907392 | bytes 42467328 | tf_op jit(solution)/shard_map/frs,fks->frk/dot_general | solution.py:11
  186.5 138.6 %reduce-scatter.2.cloned.1.call-done = f32[1,2,256,2048]{3,2,1,0:T(8,128)} async-done(((f32[1,2,256,8192]{3,2,1,0:T(8,128)}), f32[1,2,256,2048]{3,2,1,0:T(8,128)}) %reduce-scatter.2.cloned.1.call-update) | async-done | bytes 4194320 | tf_op jit(solution)/shard_map/reduce_scatter | solution.py:126
  (54 shorter events, 8.7 us)
Async XLA Ops:
  7.2 53.4 %all-gather.2.cloned.1.call-start = ((), (), s32[]{:S(2)}) async-start(), calls=%async_computation.1 | async-start | bytes 2621440 | tf_op jit(solution)/shard_map/all_gather | solution.py:108
  9.5 8.5 %collective-permute-start = (f32[1,256,256]{2,1,0:T(8,128)S(1)}, f32[1,256,256]{2,1,0:T(8,128)S(1)}, u32[]{:S(2)}, u32[]{:S(2)}) collective-permute-start(f32[1,256,256]{2,1,0:T(8,128)S(1)} %get-tuple-element.13), channel_id=1, source_target_pairs={{0,1},{1,0},{2,3},{3,2},{4,5},{5,4},{6,7},{7,6},{8,9},{9,8},{10,11... | collective-permute-start | bytes 786440 | tf_op jit(solution)/shard_map/ppermute | solution.py:90
  18.1 0.8 copy-start.3
  18.9 306.2 %reduce-scatter.2.cloned.1.call-start = ((), (), s32[]{:S(2)}) async-start(), calls=%async_computation.2 | async-start | bytes 20971520 | tf_op jit(solution)/shard_map/reduce_scatter | solution.py:126
  19.0 6.8 %collective-permute-start.3 = (f32[1,1,1,1,256,256]{5,4,3,2,1,0:T(8,128)S(1)}, f32[1,1,1,1,256,256]{5,4,3,2,1,0:T(8,128)S(1)}, u32[]{:S(2)}, u32[]{:S(2)}) collective-permute-start(f32[1,1,1,1,256,256]{5,4,3,2,1,0:T(8,128)S(1)} %get-tuple-element.12), channel_id=1, source_target_pairs={{0,24},{8,0},{16,8},{24,16},{1,25},{9,1},{17,9},{25,17},{2,26},{10... | collective-permute-start | bytes 786440 | tf_op jit(solution)/shard_map/ppermute | solution.py:60
  21.4 7.8 %collective-permute-start.4 = (f32[1,1,1,1,256,256]{5,4,3,2,1,0:T(8,128)S(1)}, f32[1,1,1,1,256,256]{5,4,3,2,1,0:T(8,128)S(1)}, u32[]{:S(2)}, u32[]{:S(2)}) collective-permute-start(f32[1,1,1,1,256,256]{5,4,3,2,1,0:T(8,128)S(1)} %get-tuple-element.12), channel_id=1, source_target_pairs={{0,8},{8,16},{16,24},{24,0},{1,9},{9,17},{17,25},{25,1},{2,10},{10... | collective-permute-start | bytes 786440 | tf_op jit(solution)/shard_map/ppermute | solution.py:60
  25.7 5.4 %collective-permute-start.5 = (f32[1,1,1,1,128,256]{5,4,3,2,1,0:T(8,128)S(1)}, f32[1,1,1,1,128,256]{5,4,3,2,1,0:T(8,128)S(1)}, u32[]{:S(2)}, u32[]{:S(2)}) collective-permute-start(f32[1,1,1,1,128,256]{5,4,3,2,1,0:T(8,128)S(1)} %slice.52), channel_id=1, source_target_pairs={{0,24},{8,0},{16,8},{24,16},{1,25},{9,1},{17,9},{25,17},{2,26},{10... | collective-permute-start | bytes 393224 | tf_op jit(solution)/shard_map/ppermute | solution.py:69
  29.2 5.1 %collective-permute-start.6 = (f32[1,1,1,1,128,256]{5,4,3,2,1,0:T(8,128)S(1)}, f32[1,1,1,1,128,256]{5,4,3,2,1,0:T(8,128)S(1)}, u32[]{:S(2)}, u32[]{:S(2)}) collective-permute-start(f32[1,1,1,1,128,256]{5,4,3,2,1,0:T(8,128)S(1)} %slice.53), channel_id=1, source_target_pairs={{0,8},{8,16},{16,24},{24,0},{1,9},{9,17},{17,25},{25,1},{2,10},{10... | collective-permute-start | bytes 393224 | tf_op jit(solution)/shard_map/ppermute | solution.py:70
  34.3 21.3 %collective-permute-start.7 = (f32[1,4,1,1,256,256]{5,4,3,2,1,0:T(8,128)S(1)}, f32[1,4,1,1,256,256]{5,4,3,2,1,0:T(8,128)}, u32[]{:S(2)}, u32[]{:S(2)}) collective-permute-start(f32[1,4,1,1,256,256]{5,4,3,2,1,0:T(8,128)S(1)} %constant_dynamic-update-slice_fusion.11), channel_id=1, source_target_pairs={{0,1},{1,0},{2,3},{3,2},{4,5},{5,4},{6,7},{7,6},{8,9},{9,8},{10,11... | collective-permute-start | bytes 3145736 | tf_op jit(solution)/shard_map/ppermute | solution.py:90
  56.9 44.5 %collective-permute-start.9 = (f32[1,4,1,2,256,256]{5,4,3,2,1,0:T(8,128)S(1)}, f32[1,4,1,2,256,256]{5,4,3,2,1,0:T(8,128)}, u32[]{:S(2)}, u32[]{:S(2)}) collective-permute-start(f32[1,4,1,2,256,256]{5,4,3,2,1,0:T(8,128)S(1)} %constant_dynamic-update-slice_fusion.9), channel_id=1, source_target_pairs={{0,6},{2,0},{4,2},{6,4},{1,7},{3,1},{5,3},{7,5},{8,14},{10,8},{12,... | collective-permute-start | bytes 6291464 | tf_op jit(solution)/shard_map/ppermute | solution.py:60
  60.5 44.1 %collective-permute-start.8 = (f32[1,4,1,2,256,256]{5,4,3,2,1,0:T(8,128)S(1)}, f32[1,4,1,2,256,256]{5,4,3,2,1,0:T(8,128)}, u32[]{:S(2)}, u32[]{:S(2)}) collective-permute-start(f32[1,4,1,2,256,256]{5,4,3,2,1,0:T(8,128)S(1)} %constant_dynamic-update-slice_fusion.9), channel_id=1, source_target_pairs={{0,2},{2,4},{4,6},{6,0},{1,3},{3,5},{5,7},{7,1},{8,10},{10,12},{12... | collective-permute-start | bytes 6291464 | tf_op jit(solution)/shard_map/ppermute | solution.py:60
  60.5 44.3 %collective-permute-start.1 = (f32[1,1,2048,256]{3,2,1,0:T(8,128)}, f32[1,1,2048,256]{3,2,1,0:T(8,128)}, u32[]{:S(2)}, u32[]{:S(2)}) collective-permute-start(f32[1,1,2048,256]{3,2,1,0:T(8,128)} %bitcast.59), channel_id=1, source_target_pairs={{0,8},{8,16},{16,24},{24,0},{1,9},{9,17},{17,25},{25,1},{2,10},{10... | collective-permute-start | bytes 6291464 | tf_op jit(solution)/shard_map/ppermute | solution.py:60
  60.6 44.3 %collective-permute-start.2 = (f32[1,1,2048,256]{3,2,1,0:T(8,128)}, f32[1,1,2048,256]{3,2,1,0:T(8,128)}, u32[]{:S(2)}, u32[]{:S(2)}) collective-permute-start(f32[1,1,2048,256]{3,2,1,0:T(8,128)} %bitcast.60), channel_id=1, source_target_pairs={{0,24},{8,0},{16,8},{24,16},{1,25},{9,1},{17,9},{25,17},{2,26},{10... | collective-permute-start | bytes 6291464 | tf_op jit(solution)/shard_map/ppermute | solution.py:60
  64.2 46.7 %copy-start.2 = (f32[1,2048,256]{2,1,0:T(8,128)S(1)}, f32[1,2048,256]{2,1,0:T(8,128)}, u32[]{:S(2)}) copy-start(f32[1,2048,256]{2,1,0:T(8,128)} %all-gather.2.cloned.1.call-done) | copy-start | bytes 6291460
  107.5 20.8 %collective-permute-start.13 = (f32[1,2,1,2,256,256]{5,4,3,2,1,0:T(8,128)S(1)}, f32[1,2,1,2,256,256]{5,4,3,2,1,0:T(8,128)S(1)}, u32[]{:S(2)}, u32[]{:S(2)}) collective-permute-start(f32[1,2,1,2,256,256]{5,4,3,2,1,0:T(8,128)S(1)} %slice.46), channel_id=1, source_target_pairs={{0,2},{2,4},{4,6},{6,0},{1,3},{3,5},{5,7},{7,1},{8,10},{10,12},{12... | collective-permute-start | bytes 3145736 | tf_op jit(solution)/shard_map/ppermute | solution.py:70
  107.6 19.7 %collective-permute-start.12 = (f32[1,2,1,2,256,256]{5,4,3,2,1,0:T(8,128)S(1)}, f32[1,2,1,2,256,256]{5,4,3,2,1,0:T(8,128)S(1)}, u32[]{:S(2)}, u32[]{:S(2)}) collective-permute-start(f32[1,2,1,2,256,256]{5,4,3,2,1,0:T(8,128)S(1)} %slice.45), channel_id=1, source_target_pairs={{0,6},{2,0},{4,2},{6,4},{1,7},{3,1},{5,3},{7,5},{8,14},{10,8},{12,... | collective-permute-start | bytes 3145736 | tf_op jit(solution)/shard_map/ppermute | solution.py:69
  113.7 26.4 %collective-permute-start.11 = (f32[1,1,1024,256]{3,2,1,0:T(8,128)S(1)}, f32[1,1,1024,256]{3,2,1,0:T(8,128)S(1)}, u32[]{:S(2)}, u32[]{:S(2)}) collective-permute-start(f32[1,1,1024,256]{3,2,1,0:T(8,128)S(1)} %slice.43), channel_id=1, source_target_pairs={{0,8},{8,16},{16,24},{24,0},{1,9},{9,17},{17,25},{25,1},{2,10},{10... | collective-permute-start | bytes 3145736 | tf_op jit(solution)/shard_map/ppermute | solution.py:70
  113.8 19.2 %collective-permute-start.10 = (f32[1,1,1024,256]{3,2,1,0:T(8,128)S(1)}, f32[1,1,1024,256]{3,2,1,0:T(8,128)S(1)}, u32[]{:S(2)}, u32[]{:S(2)}) collective-permute-start(f32[1,1,1024,256]{3,2,1,0:T(8,128)S(1)} %slice.42), channel_id=1, source_target_pairs={{0,24},{8,0},{16,8},{24,16},{1,25},{9,1},{17,9},{25,17},{2,26},{10... | collective-permute-start | bytes 3145736 | tf_op jit(solution)/shard_map/ppermute | solution.py:69
  154.2 7.1 %copy-start.1 = (f32[1,2,256,256]{3,2,1,0:T(8,128)S(1)}, f32[1,2,256,256]{3,2,1,0:T(8,128)}, u32[]{:S(2)}) copy-start(f32[1,2,256,256]{3,2,1,0:T(8,128)} %param.4) | copy-start | bytes 1572868
  161.4 11.0 %copy-start = (f32[1,2,256,256]{3,2,1,0:T(8,128)}, f32[1,2,256,256]{3,2,1,0:T(8,128)S(1)}, u32[]{:S(2)}) copy-start(f32[1,2,256,256]{3,2,1,0:T(8,128)S(1)} %fusion.24) | copy-start | bytes 1572868
Sparse Core Ops, SparseCore 0:
  19.0 33.3 all-gather.1
  186.6 138.4 reduce-scatter.1
